TPU v7x, 512 devices: a whole 4x8x8 slice. The times are simulated.
512 devices in a mesh: pairs: 128 (over y, z, core), tensor: 4 (over x).
Axes of the slice: x: 4, y: 8, z: 8, core: 2. Of those that a mesh axis runs over, the one named last changes fastest.
Arguments:
- queries: bfloat16 [32768, 4096], P('pairs', 'tensor'), may hold values from -100 to 100
- key_rows: bfloat16 [32768, 4096], P('pairs', 'tensor'), may hold values from -3.5 to 3.5
- value_rows: bfloat16 [32768, 4096], P('pairs', 'tensor'), may hold values from -12 to 12
- pair_ids: int32 [32768], P('pairs'), may hold values from 0 to 8, as said below
- out_weight: bfloat16 [4096, 4096], P('tensor', 'pairs'), may hold values from -0.09375 to 0.09375
- residual: bfloat16 [24576, 4096], P('pairs', 'tensor'), may hold values from -6 to 6
Outputs:
- hidden_out: bfloat16 [24576, 4096], P('pairs', 'tensor')
Inputs may be any that keep to these rules, and one draw needn't show every extreme that they name: `pair_ids`: within each block of 256 rows the entries never fall; rows with a value below 8 come first and rows with value 8 form the block's tail; equal values below 8 form one pair. The used rows of blocks 2k and 2k + 1 together number at most 384, reached by some two blocks, and some block has no unused row.
All inputs are finite; a program needn't handle non-finite values.
Results may differ from a plain program's by a relative error of at most 0.0055.
Values may be sent and summed in bfloat16 or wider, within the bound.
No kernel may reach another device: no remote copies, remote signals or barrier semaphores. Data moves between devices by JAX's collectives and lax.ppermute only.
A program may use at most 64 MiB of HBM per device.

v0:
```python
import jax
import jax.numpy as jnp
from jax import lax
from jax.sharding import PartitionSpec as P

HEAD = 64
SLOTS = 8


def carried_in(part, axis, combine, identity):
    place = lax.axis_index(axis)
    gathered = lax.all_gather(part, axis)
    state = jnp.zeros_like(part) + jnp.asarray(identity, part.dtype)

    def one(step, state):
        return combine(state, lax.dynamic_index_in_dim(gathered, step, 0, False))

    return lax.fori_loop(0, place, one, state)


def attend_group(query_part, key_part, value_part, allowed):
    scores = jnp.einsum("qhd,khd->hqk", query_part, key_part, preferred_element_type=jnp.float32)
    masked = jnp.where(allowed[None], scores, -1e30)
    row_top = jnp.max(masked, axis=2, keepdims=True)
    exp_terms = jnp.where(allowed[None], jnp.exp(masked - row_top), 0.0)
    row_total = jnp.maximum(jnp.sum(exp_terms, axis=2, keepdims=True), 1.0)
    weights = (exp_terms / row_total).astype(jnp.bfloat16)
    mixed = jnp.einsum("hqk,khd->qhd", weights, value_part, preferred_element_type=jnp.float32)
    return mixed.astype(jnp.bfloat16)


def add_counts(earlier, later):
    return earlier + later


def shards(queries, key_rows, value_rows, pair_ids, out_weight, residual):
    cap_rows = queries.shape[0]
    local_width = queries.shape[1]
    heads_local = local_width // HEAD
    group_size = 4
    balanced_rows = residual.shape[0]
    allowed = (pair_ids[:, None] == pair_ids[None, :]) & (pair_ids[:, None] < SLOTS)

    def split_heads(stacked):
        return stacked.reshape(cap_rows, heads_local // group_size, group_size, HEAD).transpose(
            1, 0, 2, 3
        )

    def per_group(operands):
        return attend_group(operands[0], operands[1], operands[2], allowed)

    grouped = lax.map(
        per_group, (split_heads(queries), split_heads(key_rows), split_heads(value_rows))
    )
    attended = grouped.transpose(1, 0, 2, 3).reshape(cap_rows, local_width)
    live_rows = jnp.sum((pair_ids < SLOTS).astype(jnp.int32))
    devices = lax.axis_size("pairs")
    row_start = carried_in(live_rows.reshape(1), "pairs", add_counts, jnp.zeros((1,), jnp.int32))[0]
    partial_value = jnp.dot(
        attended,
        lax.all_gather(out_weight, "pairs", axis=1, tiled=True),
        preferred_element_type=jnp.float32,
    )
    payload = lax.psum_scatter(
        partial_value.astype(jnp.bfloat16), "tensor", scatter_dimension=1, tiled=True
    )
    per_peer = cap_rows // devices
    feature_width = payload.shape[1]
    peer_index = jnp.arange(devices, dtype=jnp.int32)
    turn_index = jnp.arange(per_peer, dtype=jnp.int32)
    source_rows = ((peer_index - row_start) % devices)[:, None] + devices * turn_index[None, :]
    slot_index = jnp.where(
        source_rows < live_rows, (row_start + source_rows) // devices, balanced_rows
    ).astype(jnp.int32)
    outgoing = jnp.take(payload, source_rows.reshape(-1), axis=0).reshape(
        devices, per_peer, feature_width
    )
    incoming = lax.all_to_all(outgoing, "pairs", split_axis=0, concat_axis=0, tiled=True)
    incoming_slots = lax.all_to_all(slot_index, "pairs", split_axis=0, concat_axis=0, tiled=True)
    landed = jnp.zeros((balanced_rows, feature_width), payload.dtype)
    moved_rows = landed.at[incoming_slots.reshape(-1)].set(
        incoming.reshape(-1, feature_width), mode="drop"
    )
    return (residual.astype(jnp.float32) + moved_rows.astype(jnp.float32)).astype(jnp.bfloat16)


def solution(mesh):
    in_specs = (
        P("pairs", "tensor"),
        P("pairs", "tensor"),
        P("pairs", "tensor"),
        P("pairs"),
        P("tensor", "pairs"),
        P("pairs", "tensor"),
    )
    out_specs = P("pairs", "tensor")
    return jax.shard_map(shards, mesh=mesh, in_specs=in_specs, out_specs=out_specs, check_vma=False)
```

profile of v0, /device:TPU:6, one launch (start us, length us, event | category | flops | bytes accessed | tf_op | source)
XLA Modules:
  0.0 358.3 jit_solution(10043255233343944418)
XLA Ops:
  6.5 0.0 all-gather.2.cloned.1.call-start
  6.5 0.7 all-gather.2.cloned.1.call-update
  7.3 0.0 reduce-scatter.2.cloned.1.call-start
  7.3 1.2 copy.21
  8.6 1.2 copy.22
  9.8 1.2 copy.23
  11.1 1.4 convert_reduce_fusion
  12.4 9.2 %while.22 = (s32[]{:T(128)}, bf16[4,256,4,64]{1,3,2,0:T(8,128)(2,1)S(1)}, bf16[4,256,4,64]{1,3,2,0:T(8,128)(2,1)S(1)}, bf16[4,256,4,64]{1,3,2,0:T(8,128)(2,1)S(1...) while((s32[]{:T(128)}, ...), condition=%wide.region_6.7_spmd.clone, body=%wide.region_3.6_spmd.clone.sunk | while | flops 103221760 | bytes 1134941 | solution.py:52
  12.4 0.9 compare_and_fusion.3
  13.3 0.6 fusion.64
  13.9 0.8 fusion.65
  14.7 0.9 compare_and_fusion.3
  15.6 0.6 fusion.64
  16.2 0.8 fusion.65
  17.1 0.9 compare_and_fusion.3
  17.9 0.6 fusion.64
  18.5 0.8 fusion.65
  19.4 0.9 compare_and_fusion.3
  20.2 0.6 fusion.64
  20.9 0.8 fusion.65
  21.7 81.6 %all-gather.2.cloned.1.call-done = bf16[1024,4096]{0,1:T(8,128)(2,1)} async-done(((bf16[1024,32]{0,1:T(8,128)(2,1)}), bf16[1024,4096]{0,1:T(8,128)(2,1)}) %all-gather.2.cloned.1.call-update) | async-done | bytes 8388624 | tf_op jit(solution)/shard_map/all_gather | solution.py:61
  103.2 7.2 %convolution_convert_fusion.1 = bf16[256,4096]{1,0:T(8,128)(2,1)} fusion(bf16[256,1024]{0,1:T(8,128)(2,1)S(1)} %bitcast.75, bf16[1024,4096]{0,1:T(8,128)(2,1)} %all-gather.2.cloned.1.call-done), kind=kOutput, calls=%fused_computation.29 | convolution fusion | flops 2148532224 | bytes 11010048 | tf_op jit(solution)/shard_map/dot_general | solution.py:59
  110.4 0.0 copy-start
  110.4 0.0 reduce-scatter.2.cloned.1.call-update
  110.5 1.4 dynamic-slice
  111.9 1.4 dynamic-update-slice
  113.3 22.5 %all-reduce = s32[128]{0:T(128)S(1)} all-reduce(s32[128]{0:T(128)S(1)} %dynamic-update-slice), channel_id=1, replica_groups=mesh['pairs'=128,'tensor'=4] {'pairs'}, use_global_device_ids=true, to_apply=%add | all-reduce | flops 128 | bytes 1024
  135.8 1.7 compare_select_fusion
  137.5 171.8 %all-to-all-start = ((s32[128,1,2]{2,1,0:T(1,128)}), s32[128,1,2]{2,1,0:T(1,128)S(1)}, u32[]{:S(2)}, u32[]{:S(2)}) async-start(s32[128,1,2]{2,1,0:T(1,128)} %compare_select_fusion), calls=%async_computation | async-start | bytes 131072 | tf_op jit(solution)/shard_map/all_to_all | solution.py:79
  309.3 0.1 broadcast_add_fusion
  309.4 0.1 copy.24
  309.5 0.1 add.137
  309.7 0.1 compare_and_fusion.1
  309.7 0.1 copy.20
  309.9 0.0 reduce-scatter.2.cloned.1.call-done
  309.9 2.7 gather_fusion
  312.6 0.2 gather.7
  312.8 1.4 broadcast_select_fusion
  314.2 6.3 %all-to-all-done = s32[128,1,2]{2,1,0:T(1,128)S(1)} async-done(((s32[128,1,2]{2,1,0:T(1,128)}), s32[128,1,2]{2,1,0:T(1,128)S(1)}, u32[]{:S(2)}, u32[]{:S(2)}) %all-to-all-start) | async-done | bytes 1056 | tf_op jit(solution)/shard_map/all_to_all | solution.py:79
  320.4 7.5 %all-to-all-start.1 = ((bf16[128,2,1024]{2,1,0:T(2,128)(2,1)}), bf16[128,2,1024]{2,1,0:T(2,128)(2,1)S(1)}, u32[]{:S(2)}, u32[]{:S(2)}) async-start(bf16[128,2,1024]{2,1,0:T(2,128)(2,1)} %broadcast_select_fusion), calls=%async_computation.2 | async-start | bytes 1048576 | tf_op jit(solution)/shard_map/all_to_all | solution.py:78
  327.9 0.5 broadcast.217
  328.4 0.8 reduce.3
  329.2 0.1 reshape.216
  329.4 19.2 %all-to-all-done.1 = bf16[128,2,1024]{2,1,0:T(2,128)(2,1)S(1)} async-done(((bf16[128,2,1024]{2,1,0:T(2,128)(2,1)}), bf16[128,2,1024]{2,1,0:T(2,128)(2,1)S(1)}, u32[]{:S(2)}, u32[]{:S(2)}) %all-to-all-start.1) | async-done | bytes 524320 | tf_op jit(solution)/shard_map/all_to_all | solution.py:78
  348.6 0.2 reshape.234
  348.8 1.8 scatter_custom_fusion
  350.5 0.0 copy-done
  350.5 0.9 add_convert_fusion
  (12 shorter events, 0.1 us)
Async XLA Ops:
  6.5 96.7 %all-gather.2.cloned.1.call-start = ((), (), s32[]{:S(2)}) async-start(), calls=%async_computation.3 | async-start | bytes 8454144 | tf_op jit(solution)/shard_map/all_gather | solution.py:61
  7.3 302.7 %reduce-scatter.2.cloned.1.call-start = ((), (), s32[]{:S(2)}) async-start(), calls=%async_computation.4 | async-start | bytes 2621440 | tf_op jit(solution)/shard_map/reduce_scatter | solution.py:64
  110.4 240.1 %copy-start = (bf16[192,1024]{1,0:T(8,128)(2,1)S(1)}, bf16[192,1024]{1,0:T(8,128)(2,1)}, u32[]{:S(2)}) copy-start(bf16[192,1024]{1,0:T(8,128)(2,1)} %param.15) | copy-start | bytes 1179652
  137.5 182.9 %all-to-all-start = ((s32[128,1,2]{2,1,0:T(1,128)}), s32[128,1,2]{2,1,0:T(1,128)S(1)}, u32[]{:S(2)}, u32[]{:S(2)}) async-start(s32[128,1,2]{2,1,0:T(1,128)} %compare_select_fusion), calls=%async_computation | async-start | bytes 131072 | tf_op jit(solution)/shard_map/all_to_all | solution.py:79
  320.4 28.1 %all-to-all-start.1 = ((bf16[128,2,1024]{2,1,0:T(2,128)(2,1)}), bf16[128,2,1024]{2,1,0:T(2,128)(2,1)S(1)}, u32[]{:S(2)}, u32[]{:S(2)}) async-start(bf16[128,2,1024]{2,1,0:T(2,128)(2,1)} %broadcast_select_fusion), calls=%async_computation.2 | async-start | bytes 1048576 | tf_op jit(solution)/shard_map/all_to_all | solution.py:78
Sparse Core Ops, SparseCore 0:
  10.5 92.7 all-gather.1
  110.6 29.8 reduce-scatter.1
where the time goes:
time: 360 us; the launch traced here: 358 us
  starting transfers between devices  179 us (50%)
  waiting for transfers between devices  108 us (30%)
  blocking collectives  22.5 us (6%)
  between operations  13.5 us (4%)
  matrix products  12.9 us (4%)
  local copies, waits for them, and re-layouts  12.4 us (3%)
  other arithmetic  9.83 us (3%)
    all_to_all x1, starting transfers between devices, shards(): lax.all_to_all(slot_index, 'pairs', split_axis=0, concat_axis=0, tiled=True)  172 us
    all_gather x1, waiting for transfers between devices, shards(): lax.all_gather(out_weight, 'pairs', axis=1, tiled=True)  81.6 us
    unnamed x1, blocking collectives  22.5 us
    all_to_all x1, waiting for transfers between devices, shards(): lax.all_to_all(outgoing, 'pairs', split_axis=0, concat_axis=0, tiled=True)  19.2 us
    all_to_all x1, starting transfers between devices, shards(): lax.all_to_all(outgoing, 'pairs', split_axis=0, concat_axis=0, tiled=True)  7.48 us
    dot_general x1, matrix products, shards(): jnp.dot(attended, lax.all_gather(out_weight, 'pairs', axis=1, tiled=True)...  7.2 us
  transfers between devices with their start and end apart: 4, of which 3 were waited for; matrix products, arithmetic and copies ran while one was open for 7% of the time, Pallas kernels for 0%

commit v1 on v0

--- a/solution.py
+++ b/solution.py
@@ -7,15 +7,11 @@
 SLOTS = 8
 
 
-def carried_in(part, axis, combine, identity):
+def carried_in(part, axis):
     place = lax.axis_index(axis)
     gathered = lax.all_gather(part, axis)
-    state = jnp.zeros_like(part) + jnp.asarray(identity, part.dtype)
-
-    def one(step, state):
-        return combine(state, lax.dynamic_index_in_dim(gathered, step, 0, False))
-
-    return lax.fori_loop(0, place, one, state)
+    earlier = jnp.arange(gathered.shape[0], dtype=jnp.int32) < place
+    return jnp.sum(jnp.where(earlier, gathered, 0)), gathered
 
 
 def attend_group(query_part, key_part, value_part, allowed):
@@ -27,10 +23,6 @@
     weights = (exp_terms / row_total).astype(jnp.bfloat16)
     mixed = jnp.einsum("hqk,khd->qhd", weights, value_part, preferred_element_type=jnp.float32)
     return mixed.astype(jnp.bfloat16)
-
-
-def add_counts(earlier, later):
-    return earlier + later
 
 
 def shards(queries, key_rows, value_rows, pair_ids, out_weight, residual):
@@ -55,7 +47,8 @@
     attended = grouped.transpose(1, 0, 2, 3).reshape(cap_rows, local_width)
     live_rows = jnp.sum((pair_ids < SLOTS).astype(jnp.int32))
     devices = lax.axis_size("pairs")
-    row_start = carried_in(live_rows.reshape(1), "pairs", add_counts, jnp.zeros((1,), jnp.int32))[0]
+    row_start, all_live = carried_in(live_rows, "pairs")
+    all_start = jnp.cumsum(all_live) - all_live
     partial_value = jnp.dot(
         attended,
         lax.all_gather(out_weight, "pairs", axis=1, tiled=True),
@@ -69,14 +62,15 @@
     peer_index = jnp.arange(devices, dtype=jnp.int32)
     turn_index = jnp.arange(per_peer, dtype=jnp.int32)
     source_rows = ((peer_index - row_start) % devices)[:, None] + devices * turn_index[None, :]
-    slot_index = jnp.where(
-        source_rows < live_rows, (row_start + source_rows) // devices, balanced_rows
-    ).astype(jnp.int32)
     outgoing = jnp.take(payload, source_rows.reshape(-1), axis=0).reshape(
         devices, per_peer, feature_width
     )
     incoming = lax.all_to_all(outgoing, "pairs", split_axis=0, concat_axis=0, tiled=True)
-    incoming_slots = lax.all_to_all(slot_index, "pairs", split_axis=0, concat_axis=0, tiled=True)
+    me = lax.axis_index("pairs")
+    peer_rows = ((me - all_start) % devices)[:, None] + devices * turn_index[None, :]
+    incoming_slots = jnp.where(
+        peer_rows < all_live[:, None], (all_start[:, None] + peer_rows) // devices, balanced_rows
+    ).astype(jnp.int32)
     landed = jnp.zeros((balanced_rows, feature_width), payload.dtype)
     moved_rows = landed.at[incoming_slots.reshape(-1)].set(
         incoming.reshape(-1, feature_width), mode="drop"

time: 360 us -> 191 us (0.53)
  starting transfers between devices: 179 us -> 14.5 us
    all_to_all x1 -> x0, starting transfers between devices: 172 us -> none  [shards(): lax.all_to_all(slot_index, 'pairs', split_axis=0, concat_axis=0, tiled=True)]
    all_to_all x1, starting transfers between devices: 7.48 us -> 14.5 us  [shards(): lax.all_to_all(outgoing, 'pairs', split_axis=0, concat_axis=0, tiled=True)]
    all_to_all x1 -> x0, waiting for transfers between devices: 6.25 us -> none  [shards(): lax.all_to_all(slot_index, 'pairs', split_axis=0, concat_axis=0, tiled=True)]
  transfers between devices with their start and end apart: 4 -> 3, of which waited for: 3 -> 3; matrix products, arithmetic and copies ran while one was open for 7% -> 10% of each run, Pallas kernels for 0% -> 0%
where the time goes in v1:
time: 191 us; the launch traced here: 190 us
  waiting for transfers between devices  105 us (55%)
  blocking collectives  22.5 us (12%)
  starting transfers between devices  14.5 us (8%)
  between operations  13.5 us (7%)
  matrix products  12.9 us (7%)
  local copies, waits for them, and re-layouts  12.4 us (6%)
  other arithmetic  8.81 us (5%)
    all_gather x1, waiting for transfers between devices, shards(): lax.all_gather(out_weight, 'pairs', axis=1, tiled=True)  81.6 us
    unnamed x1, blocking collectives  22.5 us
    all_to_all x1, waiting for transfers between devices, shards(): lax.all_to_all(outgoing, 'pairs', split_axis=0, concat_axis=0, tiled=True)  20.1 us
    all_to_all x1, starting transfers between devices, shards(): lax.all_to_all(outgoing, 'pairs', split_axis=0, concat_axis=0, tiled=True)  14.5 us
    dot_general x1, matrix products, shards(): jnp.dot(attended, lax.all_gather(out_weight, 'pairs', axis=1, tiled=True)...  7.2 us
    unnamed x8, local copies, waits for them, and re-layouts  6.58 us
  transfers between devices with their start and end apart: 3, of which 3 were waited for; matrix products, arithmetic and copies ran while one was open for 10% of the time, Pallas kernels for 0%

profile of v1, /device:TPU:6, one launch (start us, length us, event | category | flops | bytes accessed | tf_op | source)
XLA Modules:
  0.0 189.6 jit_solution(13776889827314503494)
XLA Ops:
  6.5 0.0 all-gather.2.cloned.1.call-start
  6.5 0.7 all-gather.2.cloned.1.call-update
  7.3 0.0 reduce-scatter.2.cloned.1.call-start
  7.3 1.2 copy.22
  8.6 1.2 copy.23
  9.8 1.2 copy.24
  11.1 1.3 convert_reduce_fusion
  12.4 9.2 %while.11 = (s32[]{:T(128)}, bf16[4,256,4,64]{1,3,2,0:T(8,128)(2,1)S(1)}, bf16[4,256,4,64]{1,3,2,0:T(8,128)(2,1)S(1)}, bf16[4,256,4,64]{1,3,2,0:T(8,128)(2,1)S(1...) while((s32[]{:T(128)}, ...), condition=%wide.region_6.7_spmd.clone, body=%wide.region_3.6_spmd.clone.sunk | while | flops 103221760 | bytes 1134941 | solution.py:44
  12.4 0.9 compare_and_fusion.3
  13.2 0.6 fusion.66
  13.9 0.8 fusion.67
  14.7 0.9 compare_and_fusion.3
  15.6 0.6 fusion.66
  16.2 0.8 fusion.67
  17.0 0.9 compare_and_fusion.3
  17.9 0.6 fusion.66
  18.5 0.8 fusion.67
  19.3 0.9 compare_and_fusion.3
  20.2 0.6 fusion.66
  20.8 0.8 fusion.67
  21.6 81.6 %all-gather.2.cloned.1.call-done = bf16[1024,4096]{0,1:T(8,128)(2,1)} async-done(((bf16[1024,32]{0,1:T(8,128)(2,1)}), bf16[1024,4096]{0,1:T(8,128)(2,1)}) %all-gather.2.cloned.1.call-update) | async-done | bytes 8388624 | tf_op jit(solution)/shard_map/all_gather | solution.py:54
  103.2 7.2 %convolution_convert_fusion.1 = bf16[256,4096]{1,0:T(8,128)(2,1)} fusion(bf16[256,1024]{0,1:T(8,128)(2,1)S(1)} %bitcast.72, bf16[1024,4096]{0,1:T(8,128)(2,1)} %all-gather.2.cloned.1.call-done), kind=kOutput, calls=%fused_computation.28 | convolution fusion | flops 2148532224 | bytes 11010048 | tf_op jit(solution)/shard_map/dot_general | solution.py:52
  110.4 0.0 copy-start
  110.4 0.0 reduce-scatter.2.cloned.1.call-update
  110.5 1.4 dynamic-slice
  111.9 1.4 dynamic-update-slice
  113.3 22.5 %all-reduce = s32[128]{0:T(128)S(1)} all-reduce(s32[128]{0:T(128)S(1)} %dynamic-update-slice), channel_id=1, replica_groups=mesh['pairs'=128,'tensor'=4] {'pairs'}, use_global_device_ids=true, to_apply=%add | all-reduce | flops 128 | bytes 1024
  135.9 0.1 copy.18
  136.0 0.2 reduce-window.9
  136.1 0.1 reduce
  136.3 0.6 and_select_fusion.2
  136.9 0.7 and_select_fusion.1
  137.6 0.1 broadcast_add_fusion
  137.6 0.1 copy.25
  137.7 0.1 add.145
  137.9 0.1 compare_and_fusion.1
  138.0 0.1 copy.21
  138.1 2.4 %reduce-scatter.2.cloned.1.call-done = bf16[256,1024]{1,0:T(8,128)(2,1)} async-done(((bf16[256,4096]{1,0:T(8,128)(2,1)}), bf16[256,1024]{1,0:T(8,128)(2,1)}) %reduce-scatter.2.cloned.1.call-update) | async-done | bytes 524304 | tf_op jit(solution)/shard_map/reduce_scatter | solution.py:57
  140.5 2.7 %gather_fusion = bf16[256,1024]{1,0:T(8,128)(2,1)S(1)} fusion(bf16[256,1024]{1,0:T(8,128)(2,1)} %reduce-scatter.2.cloned.1.call-done, s32[1024]{0:T(1024)S(1)} %pad_clamp_fusion), kind=kCustom, calls=%fused_computation | custom fusion | bytes 1049600 | tf_op jit(solution)/shard_map/jit(_take)/gather | solution.py:65
  143.2 0.2 gather.7
  143.4 1.4 broadcast_select_fusion
  144.8 14.5 %all-to-all-start = ((bf16[128,2,1024]{2,1,0:T(2,128)(2,1)}), bf16[128,2,1024]{2,1,0:T(2,128)(2,1)S(1)}, u32[]{:S(2)}, u32[]{:S(2)}) async-start(bf16[128,2,1024]{2,1,0:T(2,128)(2,1)} %broadcast_select_fusion), calls=%async_computation.1 | async-start | bytes 1048576 | tf_op jit(solution)/shard_map/all_to_all | solution.py:68
  159.3 0.1 copy.19
  159.4 0.1 lt.81
  159.6 0.1 copy.20
  159.7 0.1 add.138
  159.8 20.1 %all-to-all-done = bf16[128,2,1024]{2,1,0:T(2,128)(2,1)S(1)} async-done(((bf16[128,2,1024]{2,1,0:T(2,128)(2,1)}), bf16[128,2,1024]{2,1,0:T(2,128)(2,1)S(1)}, u32[]{:S(2)}, u32[]{:S(2)}) %all-to-all-start) | async-done | bytes 524320 | tf_op jit(solution)/shard_map/all_to_all | solution.py:68
  179.9 0.2 reshape.239
  180.1 1.8 scatter_custom_fusion
  181.9 0.0 copy-done
  181.9 0.9 add_convert_fusion
  (10 shorter events, 0.1 us)
Async XLA Ops:
  6.5 96.7 %all-gather.2.cloned.1.call-start = ((), (), s32[]{:S(2)}) async-start(), calls=%async_computation.2 | async-start | bytes 8454144 | tf_op jit(solution)/shard_map/all_gather | solution.py:54
  7.3 133.2 %reduce-scatter.2.cloned.1.call-start = ((), (), s32[]{:S(2)}) async-start(), calls=%async_computation.3 | async-start | bytes 2621440 | tf_op jit(solution)/shard_map/reduce_scatter | solution.py:57
  110.4 71.4 %copy-start = (bf16[192,1024]{1,0:T(8,128)(2,1)S(1)}, bf16[192,1024]{1,0:T(8,128)(2,1)}, u32[]{:S(2)}) copy-start(bf16[192,1024]{1,0:T(8,128)(2,1)} %param.13) | copy-start | bytes 1179652
  144.8 35.1 %all-to-all-start = ((bf16[128,2,1024]{2,1,0:T(2,128)(2,1)}), bf16[128,2,1024]{2,1,0:T(2,128)(2,1)S(1)}, u32[]{:S(2)}, u32[]{:S(2)}) async-start(bf16[128,2,1024]{2,1,0:T(2,128)(2,1)} %broadcast_select_fusion), calls=%async_computation.1 | async-start | bytes 1048576 | tf_op jit(solution)/shard_map/all_to_all | solution.py:68
Sparse Core Ops, SparseCore 0:
  10.5 92.7 all-gather.1
  110.6 29.8 reduce-scatter.1

commit v2 on v1

--- a/solution.py
+++ b/solution.py
@@ -49,21 +49,12 @@
     devices = lax.axis_size("pairs")
     row_start, all_live = carried_in(live_rows, "pairs")
     all_start = jnp.cumsum(all_live) - all_live
-    partial_value = jnp.dot(
-        attended,
-        lax.all_gather(out_weight, "pairs", axis=1, tiled=True),
-        preferred_element_type=jnp.float32,
-    )
-    payload = lax.psum_scatter(
-        partial_value.astype(jnp.bfloat16), "tensor", scatter_dimension=1, tiled=True
-    )
     per_peer = cap_rows // devices
-    feature_width = payload.shape[1]
     peer_index = jnp.arange(devices, dtype=jnp.int32)
     turn_index = jnp.arange(per_peer, dtype=jnp.int32)
     source_rows = ((peer_index - row_start) % devices)[:, None] + devices * turn_index[None, :]
-    outgoing = jnp.take(payload, source_rows.reshape(-1), axis=0).reshape(
-        devices, per_peer, feature_width
+    outgoing = jnp.take(attended, source_rows.reshape(-1), axis=0).reshape(
+        devices, per_peer, local_width
     )
     incoming = lax.all_to_all(outgoing, "pairs", split_axis=0, concat_axis=0, tiled=True)
     me = lax.axis_index("pairs")
@@ -71,11 +62,19 @@
     incoming_slots = jnp.where(
         peer_rows < all_live[:, None], (all_start[:, None] + peer_rows) // devices, balanced_rows
     ).astype(jnp.int32)
-    landed = jnp.zeros((balanced_rows, feature_width), payload.dtype)
+    landed = jnp.zeros((balanced_rows, local_width), attended.dtype)
     moved_rows = landed.at[incoming_slots.reshape(-1)].set(
-        incoming.reshape(-1, feature_width), mode="drop"
+        incoming.reshape(-1, local_width), mode="drop"
     )
-    return (residual.astype(jnp.float32) + moved_rows.astype(jnp.float32)).astype(jnp.bfloat16)
+    partial_value = jnp.dot(
+        moved_rows,
+        lax.all_gather(out_weight, "pairs", axis=1, tiled=True),
+        preferred_element_type=jnp.float32,
+    )
+    payload = lax.psum_scatter(
+        partial_value.astype(jnp.bfloat16), "tensor", scatter_dimension=1, tiled=True
+    )
+    return (residual.astype(jnp.float32) + payload.astype(jnp.float32)).astype(jnp.bfloat16)
 
 
 def solution(mesh):

time: 191 us -> 156 us (0.82)
  waiting for transfers between devices: 105 us -> 68.2 us
  blocking collectives: 22.5 us -> 31.6 us
  starting transfers between devices: 14.5 us -> 6.83 us
    all_gather x1, waiting for transfers between devices: 81.6 us -> 16.4 us  [shards(): lax.all_gather(out_weight, 'pairs', axis=1, tiled=True)]
    reduce_scatter x1, waiting for transfers between devices: 2.38 us -> 27.2 us  [shards(): lax.psum_scatter(partial_value.astype(jnp.bfloat16), 'tensor', scatter_di...]
    unnamed x1, blocking collectives: 22.5 us -> 31.6 us
    all_to_all x1, starting transfers between devices: 14.5 us -> 6.78 us  [shards(): lax.all_to_all(outgoing, 'pairs', split_axis=0, concat_axis=0, tiled=True)]
    all_to_all x1, waiting for transfers between devices: 20.1 us -> 23.8 us  [shards(): lax.all_to_all(outgoing, 'pairs', split_axis=0, concat_axis=0, tiled=True)]
  transfers between devices with their start and end apart: 3 -> 3, of which waited for: 3 -> 3; matrix products, arithmetic and copies ran while one was open for 10% -> 16% of each run, Pallas kernels for 0% -> 0%
where the time goes in v2:
time: 156 us; the launch traced here: 154 us
  waiting for transfers between devices  68.2 us (44%)
  blocking collectives  31.6 us (20%)
  between operations  13.5 us (9%)
  matrix products  13.2 us (8%)
  local copies, waits for them, and re-layouts  10.9 us (7%)
  other arithmetic  9.73 us (6%)
  starting transfers between devices  6.83 us (4%)
    unnamed x1, blocking collectives  31.6 us
    reduce_scatter x1, waiting for transfers between devices, shards(): lax.psum_scatter(partial_value.astype(jnp.bfloat16), 'tensor', scatter_di...  27.2 us
    all_to_all x1, waiting for transfers between devices, shards(): lax.all_to_all(outgoing, 'pairs', split_axis=0, concat_axis=0, tiled=True)  23.8 us
    all_gather x1, waiting for transfers between devices, shards(): lax.all_gather(out_weight, 'pairs', axis=1, tiled=True)  16.4 us
    dot_general x1, matrix products, shards(): jnp.dot(moved_rows, lax.all_gather(out_weight, 'pairs', axis=1, tiled=Tru...  7.53 us
    all_to_all x1, starting transfers between devices, shards(): lax.all_to_all(outgoing, 'pairs', split_axis=0, concat_axis=0, tiled=True)  6.78 us
    unnamed x8, local copies, waits for them, and re-layouts  6.33 us
    and x4, other arithmetic, shards(): (pair_ids[:, None] == pair_ids[None, :]) & (pair_ids[:, None] < SLOTS)  3.46 us
  transfers between devices with their start and end apart: 3, of which 3 were waited for; matrix products, arithmetic and copies ran while one was open for 16% of the time, Pallas kernels for 0%

profile of v2, /device:TPU:6, one launch (start us, length us, event | category | flops | bytes accessed | tf_op | source)
XLA Modules:
  0.0 154.1 jit_solution(11012819617833338367)
XLA Ops:
  6.5 0.0 all-gather.2.cloned.1.call-start
  6.5 0.7 all-gather.2.cloned.1.call-update
  7.3 1.3 dynamic-slice
  8.6 1.3 convert_reduce_fusion
  9.9 1.3 dynamic-update-slice
  11.2 31.6 %all-reduce = s32[128]{0:T(128)S(1)} all-reduce(s32[128]{0:T(128)S(1)} %dynamic-update-slice), channel_id=1, replica_groups=mesh['pairs'=128,'tensor'=4] {'pairs'}, use_global_device_ids=true, to_apply=%add | all-reduce | flops 128 | bytes 1024
  42.8 0.1 copy.20
  42.9 0.2 reduce-window.9
  43.1 0.1 reduce
  43.2 0.6 and_select_fusion.2
  43.8 0.6 and_select_fusion.1
  44.4 0.1 broadcast_add_fusion
  44.4 0.1 copy.27
  44.6 0.1 add.145
  44.7 1.3 copy.24
  45.9 1.2 copy.25
  47.2 1.2 copy.26
  48.4 9.2 %while.11 = (s32[]{:T(128)}, bf16[4,256,4,64]{1,3,2,0:T(8,128)(2,1)S(1)}, bf16[4,256,4,64]{1,3,2,0:T(8,128)(2,1)S(1)}, bf16[4,256,4,64]{1,3,2,0:T(8,128)(2,1)S(1...) while((s32[]{:T(128)}, ...), condition=%wide.region_6.7_spmd.clone, body=%wide.region_3.6_spmd.clone.sunk | while | flops 103221760 | bytes 1134933 | solution.py:44
  48.5 0.9 compare_and_fusion.3
  49.3 0.6 fusion.66
  50.0 0.8 fusion.67
  50.8 0.9 compare_and_fusion.3
  51.6 0.6 fusion.66
  52.3 0.8 fusion.67
  53.1 0.9 compare_and_fusion.3
  53.9 0.6 fusion.66
  54.6 0.8 fusion.67
  55.4 0.9 compare_and_fusion.3
  56.3 0.6 fusion.66
  56.9 0.8 fusion.67
  57.7 0.2 copy.28
  57.9 1.2 gather_fusion
  59.1 0.0 copy-start
  59.1 0.2 gather.7
  59.3 0.1 compare_and_fusion.1
  59.4 0.1 copy.23
  59.5 1.4 broadcast_select_fusion
  61.0 6.8 %all-to-all-start = ((bf16[128,2,1024]{2,1,0:T(2,128)(2,1)}), bf16[128,2,1024]{2,1,0:T(2,128)(2,1)S(1)}, u32[]{:S(2)}, u32[]{:S(2)}) async-start(bf16[128,2,1024]{2,1,0:T(2,128)(2,1)} %broadcast_select_fusion), calls=%async_computation | async-start | bytes 1048576 | tf_op jit(solution)/shard_map/all_to_all | solution.py:59
  67.8 0.0 reduce-scatter.2.cloned.1.call-start
  67.8 0.1 copy.22
  67.9 0.1 add.138
  68.1 0.1 copy.21
  68.2 0.2 lt.81
  68.4 23.8 %all-to-all-done = bf16[128,2,1024]{2,1,0:T(2,128)(2,1)S(1)} async-done(((bf16[128,2,1024]{2,1,0:T(2,128)(2,1)}), bf16[128,2,1024]{2,1,0:T(2,128)(2,1)S(1)}, u32[]{:S(2)}, u32[]{:S(2)}) %all-to-all-start) | async-done | bytes 524320 | tf_op jit(solution)/shard_map/all_to_all | solution.py:59
  92.2 0.2 reshape.239
  92.4 1.8 %scatter_custom_fusion = bf16[192,1024]{1,0:T(8,128)(2,1)S(1)} fusion(s32[256]{0:T(256)S(1)} %bitcast.72, bf16[256,1024]{1,0:T(8,128)(2,1)S(1)} %reshape.239, bf16[]{:T(256)} %constant.74.clone.1), kind=kCustom, calls=%fused_computation.31 | custom fusion | bytes 393218 | tf_op jit(solution)/shard_map/scatter | solution.py:66
  94.1 16.4 %all-gather.2.cloned.1.call-done = bf16[1024,4096]{0,1:T(8,128)(2,1)} async-done(((bf16[1024,32]{0,1:T(8,128)(2,1)}), bf16[1024,4096]{0,1:T(8,128)(2,1)}) %all-gather.2.cloned.1.call-update) | async-done | bytes 8388624 | tf_op jit(solution)/shard_map/all_gather | solution.py:71
  110.6 7.5 %convolution_convert_fusion.1 = bf16[192,4096]{1,0:T(8,128)(2,1)} fusion(bf16[192,1024]{1,0:T(8,128)(2,1)S(1)} %scatter_custom_fusion, bf16[1024,4096]{0,1:T(8,128)(2,1)} %all-gather.2.cloned.1.call-done), kind=kOutput, calls=%fused_computation.28 | convolution fusion | flops 1611399168 | bytes 10354688 | tf_op jit(solution)/shard_map/dot_general | solution.py:69
  118.1 0.0 reduce-scatter.2.cloned.1.call-update
  118.1 27.2 %reduce-scatter.2.cloned.1.call-done = bf16[192,1024]{1,0:T(8,128)(2,1)} async-done(((bf16[192,4096]{1,0:T(8,128)(2,1)}), bf16[192,1024]{1,0:T(8,128)(2,1)}) %reduce-scatter.2.cloned.1.call-update) | async-done | bytes 393232 | tf_op jit(solution)/shard_map/reduce_scatter | solution.py:74
  145.4 0.0 copy-done
  145.4 1.9 %add_convert_fusion = bf16[192,1024]{1,0:T(8,128)(2,1)} fusion(bf16[192,1024]{1,0:T(8,128)(2,1)} %reduce-scatter.2.cloned.1.call-done, bf16[192,1024]{1,0:T(8,128)(2,1)S(1)} %copy-done), kind=kLoop, calls=%fused_computation.30 | loop fusion | flops 786432 | bytes 1179648 | tf_op jit(solution)/shard_map/convert_element_type | solution.py:77
  (10 shorter events, 0.1 us)
Async XLA Ops:
  6.5 104.0 %all-gather.2.cloned.1.call-start = ((), (), s32[]{:S(2)}) async-start(), calls=%async_computation.2 | async-start | bytes 8454144 | tf_op jit(solution)/shard_map/all_gather | solution.py:71
  59.1 86.3 %copy-start = (bf16[192,1024]{1,0:T(8,128)(2,1)S(1)}, bf16[192,1024]{1,0:T(8,128)(2,1)}, u32[]{:S(2)}) copy-start(bf16[192,1024]{1,0:T(8,128)(2,1)} %param.13) | copy-start | bytes 1179652
  61.0 31.2 %all-to-all-start = ((bf16[128,2,1024]{2,1,0:T(2,128)(2,1)}), bf16[128,2,1024]{2,1,0:T(2,128)(2,1)S(1)}, u32[]{:S(2)}, u32[]{:S(2)}) async-start(bf16[128,2,1024]{2,1,0:T(2,128)(2,1)} %broadcast_select_fusion), calls=%async_computation | async-start | bytes 1048576 | tf_op jit(solution)/shard_map/all_to_all | solution.py:59
  67.8 77.6 %reduce-scatter.2.cloned.1.call-start = ((), (), s32[]{:S(2)}) async-start(), calls=%async_computation.3 | async-start | bytes 1966080 | tf_op jit(solution)/shard_map/reduce_scatter | solution.py:74
Sparse Core Ops, SparseCore 0:
  10.5 100.0 all-gather.1
  118.2 27.0 reduce-scatter.1

commit v3 on v2

--- a/solution.py
+++ b/solution.py
@@ -8,7 +8,7 @@
 
 
 def carried_in(part, axis):
-    place = lax.axis_index(axis)
+    place = lax.axis_index(axis[0]) * lax.axis_size(axis[1]) + lax.axis_index(axis[1])
     gathered = lax.all_gather(part, axis)
     earlier = jnp.arange(gathered.shape[0], dtype=jnp.int32) < place
     return jnp.sum(jnp.where(earlier, gathered, 0)), gathered
@@ -46,8 +46,8 @@
     )
     attended = grouped.transpose(1, 0, 2, 3).reshape(cap_rows, local_width)
     live_rows = jnp.sum((pair_ids < SLOTS).astype(jnp.int32))
-    devices = lax.axis_size("pairs")
-    row_start, all_live = carried_in(live_rows, "pairs")
+    devices = lax.axis_size("chip") * lax.axis_size("core")
+    row_start, all_live = carried_in(live_rows, ("chip", "core"))
     all_start = jnp.cumsum(all_live) - all_live
     per_peer = cap_rows // devices
     peer_index = jnp.arange(devices, dtype=jnp.int32)
@@ -56,8 +56,8 @@
     outgoing = jnp.take(attended, source_rows.reshape(-1), axis=0).reshape(
         devices, per_peer, local_width
     )
-    incoming = lax.all_to_all(outgoing, "pairs", split_axis=0, concat_axis=0, tiled=True)
-    me = lax.axis_index("pairs")
+    incoming = lax.all_to_all(outgoing, ("chip", "core"), split_axis=0, concat_axis=0, tiled=True)
+    me = lax.axis_index("chip") * lax.axis_size("core") + lax.axis_index("core")
     peer_rows = ((me - all_start) % devices)[:, None] + devices * turn_index[None, :]
     incoming_slots = jnp.where(
         peer_rows < all_live[:, None], (all_start[:, None] + peer_rows) // devices, balanced_rows
@@ -66,25 +66,38 @@
     moved_rows = landed.at[incoming_slots.reshape(-1)].set(
         incoming.reshape(-1, local_width), mode="drop"
     )
-    partial_value = jnp.dot(
+    cores = lax.axis_size("core")
+    chips = devices // cores
+    stripe = out_weight.shape[1]
+    same_core = lax.all_gather(out_weight, "chip", axis=1, tiled=True)
+    both_cores = lax.all_gather(same_core, "core")
+    partial_value = jnp.einsum(
+        "rk,ckmj->rmcj",
         moved_rows,
-        lax.all_gather(out_weight, "pairs", axis=1, tiled=True),
+        both_cores.reshape(cores, -1, chips, stripe),
         preferred_element_type=jnp.float32,
-    )
+    ).astype(jnp.bfloat16)
     payload = lax.psum_scatter(
-        partial_value.astype(jnp.bfloat16), "tensor", scatter_dimension=1, tiled=True
+        partial_value.reshape(balanced_rows, -1), "tensor", scatter_dimension=1, tiled=True
     )
     return (residual.astype(jnp.float32) + payload.astype(jnp.float32)).astype(jnp.bfloat16)
 
 
 def solution(mesh):
+    pairs_size, tensor_size = mesh.devices.shape
+    split_mesh = jax.sharding.Mesh(
+        mesh.devices.reshape(pairs_size // 2, 2, tensor_size), ("chip", "core", "tensor")
+    )
+    rows = ("chip", "core")
     in_specs = (
-        P("pairs", "tensor"),
-        P("pairs", "tensor"),
-        P("pairs", "tensor"),
-        P("pairs"),
-        P("tensor", "pairs"),
-        P("pairs", "tensor"),
+        P(rows, "tensor"),
+        P(rows, "tensor"),
+        P(rows, "tensor"),
+        P(rows),
+        P("tensor", rows),
+        P(rows, "tensor"),
     )
-    out_specs = P("pairs", "tensor")
-    return jax.shard_map(shards, mesh=mesh, in_specs=in_specs, out_specs=out_specs, check_vma=False)
+    out_specs = P(rows, "tensor")
+    return jax.shard_map(
+        shards, mesh=split_mesh, in_specs=in_specs, out_specs=out_specs, check_vma=False
+    )

time: 156 us -> 244 us (1.56)
  waiting for transfers between devices: 68.2 us -> 138 us
  local copies, waits for them, and re-layouts: 10.9 us -> 29.7 us
  blocking collectives: 31.6 us -> 22.6 us
  matrix products: 13.2 us -> 18.5 us
  starting transfers between devices: 6.83 us -> 10.1 us
    all_gather x1 -> x2, waiting for transfers between devices: 16.4 us -> 94.8 us  [the longest x1 94.8 us: shards(): same_core = lax.all_gather(out_weight, 'chip', axis=1, tiled=True)]
    reshape x0 -> x2, local copies, waits for them, and re-layouts: none -> 17.2 us  [the longest x1 14.5 us: shards(): both_cores.reshape(cores, -1, chips, stripe)]
    unnamed x1, blocking collectives: 31.6 us -> 22.6 us
    dot_general x1, matrix products: 7.53 us -> 12.9 us  [shards(): jnp.einsum('rk,ckmj->rmcj', moved_rows, both_cores.reshape(cores, -1, chi...]
    reduce_scatter x1, waiting for transfers between devices: 27.2 us -> 22.4 us  [shards(): lax.psum_scatter(partial_value.reshape(balanced_rows, -1), 'tensor', scat...]
    all_to_all x1, waiting for transfers between devices: 23.8 us -> 20 us  [shards(): lax.all_to_all(outgoing, ('chip', 'core'), split_axis=0, concat_axis=0, t...]
    all_to_all x1, starting transfers between devices: 6.78 us -> 10 us  [shards(): lax.all_to_all(outgoing, ('chip', 'core'), split_axis=0, concat_axis=0, t...]
  transfers between devices with their start and end apart: 3 -> 4, of which waited for: 3 -> 3; matrix products, arithmetic and copies ran while one was open for 16% -> 10% of each run, Pallas kernels for 0% -> 0%
where the time goes in v3:
time: 244 us; the launch traced here: 242 us
  waiting for transfers between devices  138 us (57%)
  local copies, waits for them, and re-layouts  29.7 us (12%)
  blocking collectives  22.6 us (9%)
  matrix products  18.5 us (8%)
  between operations  13.3 us (5%)
  starting transfers between devices  10.1 us (4%)
  other arithmetic  9.86 us (4%)
    all_gather x1, waiting for transfers between devices, shards(): same_core = lax.all_gather(out_weight, 'chip', axis=1, tiled=True)  94.8 us
    unnamed x1, blocking collectives  22.6 us
    reduce_scatter x1, waiting for transfers between devices, shards(): lax.psum_scatter(partial_value.reshape(balanced_rows, -1), 'tensor', scat...  22.4 us
    all_to_all x1, waiting for transfers between devices, shards(): lax.all_to_all(outgoing, ('chip', 'core'), split_axis=0, concat_axis=0, t...  20 us
    reshape x1, local copies, waits for them, and re-layouts, shards(): both_cores.reshape(cores, -1, chips, stripe)  14.5 us
    dot_general x1, matrix products, shards(): jnp.einsum('rk,ckmj->rmcj', moved_rows, both_cores.reshape(cores, -1, chi...  12.9 us
    all_to_all x1, starting transfers between devices, shards(): lax.all_to_all(outgoing, ('chip', 'core'), split_axis=0, concat_axis=0, t...  10 us
    unnamed x8, local copies, waits for them, and re-layouts  6.47 us
  transfers between devices with their start and end apart: 4, of which 3 were waited for; matrix products, arithmetic and copies ran while one was open for 10% of the time, Pallas kernels for 0%

profile of v3, /device:TPU:6, one launch (start us, length us, event | category | flops | bytes accessed | tf_op | source)
XLA Modules:
  0.0 242.1 jit_solution(13406243478582322435)
XLA Ops:
  6.5 0.0 all-gather.4.cloned.1.call-start
  6.5 0.7 all-gather.4.cloned.1.call-update
  7.3 0.0 all-gather.6.cloned.1.call-start
  7.3 94.8 %all-gather.4.cloned.1.call-done = bf16[1024,2048]{0,1:T(8,128)(2,1)} async-done(((bf16[1024,32]{0,1:T(8,128)(2,1)}), bf16[1024,2048]{0,1:T(8,128)(2,1)}) %all-gather.4.cloned.1.call-update) | async-done | bytes 4194320 | tf_op jit(solution)/shard_map/all_gather | solution.py:72
  102.1 0.0 all-gather.6.cloned.1.call-update
  102.2 1.3 dynamic-slice
  103.5 1.3 convert_reduce_fusion
  104.9 1.4 dynamic-update-slice
  106.3 22.6 %all-reduce = s32[128]{0:T(128)S(1)} all-reduce(s32[128]{0:T(128)S(1)} %dynamic-update-slice), channel_id=1, replica_groups=mesh['chip'=64,'core'=2,'tensor'=4] {'chip','core'}, use_global_device_ids=true, to_apply=%add | all-reduce | flops 128 | bytes 1024
  128.9 0.1 copy.24
  129.0 0.2 reduce-window.9
  129.1 0.1 reduce
  129.3 1.3 copy.28
  130.5 1.2 copy.29
  131.8 1.2 copy.30
  133.0 9.2 %while.11 = (s32[]{:T(128)}, bf16[4,256,4,64]{1,3,2,0:T(8,128)(2,1)S(1)}, bf16[4,256,4,64]{1,3,2,0:T(8,128)(2,1)S(1)}, bf16[4,256,4,64]{1,3,2,0:T(8,128)(2,1)S(1...) while((s32[]{:T(128)}, ...), condition=%wide.region_6.7_spmd.clone, body=%wide.region_3.6_spmd.clone.sunk | while | flops 103221760 | bytes 1134941 | solution.py:44
  133.0 0.9 compare_and_fusion.3
  133.9 0.6 fusion.69
  134.5 0.8 fusion.70
  135.3 0.9 compare_and_fusion.3
  136.2 0.6 fusion.69
  136.8 0.8 fusion.70
  137.6 0.9 compare_and_fusion.3
  138.5 0.6 fusion.69
  139.1 0.8 fusion.70
  139.9 0.9 compare_and_fusion.3
  140.8 0.6 fusion.69
  141.4 0.8 fusion.70
  142.2 0.2 copy.32
  142.5 0.6 and_select_fusion.2
  143.1 0.7 and_select_fusion.1
  143.8 0.1 broadcast_add_fusion
  143.8 0.1 copy.31
  143.9 0.1 add.150
  144.1 1.2 gather_fusion
  145.3 0.2 gather.7
  145.5 0.1 compare_and_fusion.1
  145.6 0.1 copy.27
  145.7 1.4 broadcast_select_fusion
  147.1 10.0 %all-to-all-start = ((bf16[128,2,1024]{2,1,0:T(2,128)(2,1)}), bf16[128,2,1024]{2,1,0:T(2,128)(2,1)S(1)}, u32[]{:S(2)}, u32[]{:S(2)}) async-start(bf16[128,2,1024]{2,1,0:T(2,128)(2,1)} %broadcast_select_fusion), calls=%async_computation | async-start | bytes 1048576 | tf_op jit(solution)/shard_map/all_to_all | solution.py:59
  157.1 0.0 reduce-scatter.2.cloned.1.call-start
  157.2 0.1 copy.25
  157.3 0.1 lt.81
  157.5 0.1 copy.26
  157.6 0.1 add.143
  157.7 20.0 %all-to-all-done = bf16[128,2,1024]{2,1,0:T(2,128)(2,1)S(1)} async-done(((bf16[128,2,1024]{2,1,0:T(2,128)(2,1)}), bf16[128,2,1024]{2,1,0:T(2,128)(2,1)S(1)}, u32[]{:S(2)}, u32[]{:S(2)}) %all-to-all-start) | async-done | bytes 524320 | tf_op jit(solution)/shard_map/all_to_all | solution.py:59
  177.8 0.2 reshape.247
  178.0 1.9 scatter_custom_fusion
  179.9 0.0 all-gather.6.cloned.1.call-done
  179.9 14.5 %reshape.233 = bf16[2,1024,64,32]{1,0,3,2:T(2,128)(2,1)} reshape(bf16[2048,2048]{0,1:T(8,128)(2,1)} %all-gather.6.cloned.1.call-done) | data formatting | bytes 16777216 | tf_op jit(solution)/shard_map/reshape | solution.py:77
  194.4 12.9 %convert_bitcast_fusion = bf16[192,64,2,32]{0,1,3,2:T(8,128)(2,1)S(1)} fusion(bf16[2,1024,64,32]{1,0,3,2:T(2,128)(2,1)} %reshape.233, bf16[192,1024]{1,0:T(8,128)(2,1)S(1)} %scatter_custom_fusion), kind=kOutput, calls=%fused_computation.30 | convolution fusion | flops 1611399168 | bytes 10354688 | tf_op jit(solution)/shard_map/rk,ckmj->rmcj/dot_general | solution.py:74
  207.3 0.0 copy-start
  207.4 1.2 copy.34
  208.6 2.7 %copy.35 = bf16[192,4096]{1,0:T(8,128)(2,1)} copy(bf16[192,4096]{0,1:T(8,128)(2,1)S(1)} %bitcast.74) | data formatting | bytes 3145728 | tf_op jit(solution)/shard_map/reshape | solution.py:81
  211.3 0.0 reduce-scatter.2.cloned.1.call-update
  211.3 22.4 %reduce-scatter.2.cloned.1.call-done = bf16[192,1024]{1,0:T(8,128)(2,1)} async-done(((bf16[192,4096]{1,0:T(8,128)(2,1)}), bf16[192,1024]{1,0:T(8,128)(2,1)}) %reduce-scatter.2.cloned.1.call-update) | async-done | bytes 393232 | tf_op jit(solution)/shard_map/reduce_scatter | solution.py:80
  233.7 0.0 copy-done
  233.7 1.9 add_convert_fusion
  (10 shorter events, 0.1 us)
Async XLA Ops:
  6.5 95.6 %all-gather.4.cloned.1.call-start = ((), (), s32[]{:S(2)}) async-start(), calls=%async_computation.2 | async-start | bytes 4259840 | tf_op jit(solution)/shard_map/all_gather | solution.py:72
  7.3 172.7 %all-gather.6.cloned.1.call-start = ((), (), s32[]{:S(2)}) async-start(), calls=%async_computation.4 | async-start | bytes 12582912 | tf_op jit(solution)/shard_map/all_gather | solution.py:73
  147.1 30.6 %all-to-all-start = ((bf16[128,2,1024]{2,1,0:T(2,128)(2,1)}), bf16[128,2,1024]{2,1,0:T(2,128)(2,1)S(1)}, u32[]{:S(2)}, u32[]{:S(2)}) async-start(bf16[128,2,1024]{2,1,0:T(2,128)(2,1)} %broadcast_select_fusion), calls=%async_computation | async-start | bytes 1048576 | tf_op jit(solution)/shard_map/all_to_all | solution.py:59
  157.1 76.6 %reduce-scatter.2.cloned.1.call-start = ((), (), s32[]{:S(2)}) async-start(), calls=%async_computation.3 | async-start | bytes 1966080 | tf_op jit(solution)/shard_map/reduce_scatter | solution.py:80
  207.3 26.4 %copy-start = (bf16[192,1024]{1,0:T(8,128)(2,1)S(1)}, bf16[192,1024]{1,0:T(8,128)(2,1)}, u32[]{:S(2)}) copy-start(bf16[192,1024]{1,0:T(8,128)(2,1)} %param.13) | copy-start | bytes 1179652
Sparse Core Ops, SparseCore 0:
  10.4 91.7 all-gather.3
  104.2 24.6 all-gather.5
  211.4 22.2 reduce-scatter.1

commit v4 on v2

--- a/solution.py
+++ b/solution.py
@@ -71,10 +71,15 @@
         lax.all_gather(out_weight, "pairs", axis=1, tiled=True),
         preferred_element_type=jnp.float32,
     )
-    payload = lax.psum_scatter(
-        partial_value.astype(jnp.bfloat16), "tensor", scatter_dimension=1, tiled=True
+    tensor_parts = lax.axis_size("tensor")
+    by_group = (
+        partial_value.astype(jnp.bfloat16)
+        .reshape(balanced_rows, tensor_parts, local_width)
+        .transpose(1, 0, 2)
     )
-    return (residual.astype(jnp.float32) + payload.astype(jnp.float32)).astype(jnp.bfloat16)
+    received = lax.all_to_all(by_group, "tensor", 0, 0, tiled=True)
+    projected = jnp.sum(received.astype(jnp.float32), axis=0).astype(jnp.bfloat16)
+    return (residual.astype(jnp.float32) + projected.astype(jnp.float32)).astype(jnp.bfloat16)
 
 
 def solution(mesh):

time: 156 us -> 149 us (0.955)
  waiting for transfers between devices: 68.2 us -> 41.6 us
  blocking collectives: 31.6 us -> 55.4 us
  other arithmetic: 9.73 us -> 6.04 us
    reduce_scatter x1 -> x0, waiting for transfers between devices: 27.2 us -> none  [shards(): lax.psum_scatter(partial_value.astype(jnp.bfloat16), 'tensor', scatter_di...]
    all_to_all x0 -> x1, blocking collectives: none -> 23.8 us  [shards(): received = lax.all_to_all(by_group, 'tensor', 0, 0, tiled=True)]
    and x4, other arithmetic: 3.46 us -> 0.44 us  [shards(): (pair_ids[:, None] == pair_ids[None, :]) & (pair_ids[:, None] < SLOTS)]
    all_gather x1, waiting for transfers between devices: 16.4 us -> 18.4 us  [shards(): lax.all_gather(out_weight, 'pairs', axis=1, tiled=True)]
    unnamed x8 -> x10, local copies, waits for them, and re-layouts: 6.33 us -> 6.34 us
  transfers between devices with their start and end apart: 3 -> 2, of which waited for: 3 -> 2; matrix products, arithmetic and copies ran while one was open for 16% -> 15% of each run, Pallas kernels for 0% -> 0%
where the time goes in v4:
time: 149 us; the launch traced here: 146 us
  blocking collectives  55.4 us (37%)
  waiting for transfers between devices  41.6 us (28%)
  between operations  13.6 us (9%)
  matrix products  11.9 us (8%)
  local copies, waits for them, and re-layouts  11 us (7%)
  starting transfers between devices  6.79 us (5%)
  other arithmetic  6.04 us (4%)
    unnamed x1, blocking collectives  31.6 us
    all_to_all x1, blocking collectives, shards(): received = lax.all_to_all(by_group, 'tensor', 0, 0, tiled=True)  23.8 us
    all_to_all x1, waiting for transfers between devices, shards(): lax.all_to_all(outgoing, 'pairs', split_axis=0, concat_axis=0, tiled=True)  22.5 us
    all_gather x1, waiting for transfers between devices, shards(): lax.all_gather(out_weight, 'pairs', axis=1, tiled=True)  18.4 us
    all_to_all x1, starting transfers between devices, shards(): lax.all_to_all(outgoing, 'pairs', split_axis=0, concat_axis=0, tiled=True)  6.78 us
    unnamed x10, local copies, waits for them, and re-layouts  6.34 us
    dot_general x1, matrix products, shards(): jnp.dot(moved_rows, lax.all_gather(out_weight, 'pairs', axis=1, tiled=Tru...  6.27 us
    dot_general x4, matrix products, attend_group(): jnp.einsum('hqk,khd->qhd', weights, value_part, preferred_element_type=jn...  3.19 us
  transfers between devices with their start and end apart: 2, of which 2 were waited for; matrix products, arithmetic and copies ran while one was open for 15% of the time, Pallas kernels for 0%

profile of v4, /device:TPU:6, one launch (start us, length us, event | category | flops | bytes accessed | tf_op | source)
XLA Modules:
  0.0 146.4 jit_solution(11260538859287484792)
XLA Ops:
  6.5 0.0 copy-start.1
  6.5 0.0 all-gather.2.cloned.1.call-start
  6.5 0.7 all-gather.2.cloned.1.call-update
  7.3 1.3 dynamic-slice
  8.6 1.3 convert_reduce_fusion
  9.9 1.3 dynamic-update-slice
  11.2 31.6 %all-reduce = s32[128]{0:T(128)S(1)} all-reduce(s32[128]{0:T(128)S(1)} %dynamic-update-slice), channel_id=1, replica_groups=mesh['pairs'=128,'tensor'=4] {'pairs'}, use_global_device_ids=true, to_apply=%add | all-reduce | flops 128 | bytes 1024
  42.8 0.1 copy.27
  42.9 0.2 reduce-window.9
  43.1 0.1 reduce.1
  43.2 0.6 and_select_fusion.2
  43.8 0.6 and_select_fusion.1
  44.4 0.1 broadcast_add_fusion
  44.4 0.1 copy.34
  44.6 0.1 add.143
  44.7 1.3 copy.31
  45.9 1.2 copy.32
  47.2 1.2 copy.33
  48.4 0.0 copy-done.1
  48.5 6.2 %while.11 = (s32[]{:T(128)}, bf16[4,256,4,64]{1,3,2,0:T(8,128)(2,1)S(1)}, bf16[4,256,4,64]{1,3,2,0:T(8,128)(2,1)S(1)}, bf16[4,256,4,64]{1,3,2,0:T(8,128)(2,1)S(1...) while((s32[]{:T(128)}, ...), condition=%wide.region_6.7_spmd.clone, body=%wide.region_3.6_spmd.clone.sunk | while | flops 103221760 | bytes 1134933 | solution.py:44
  48.5 0.1 compare_and_fusion.3
  48.6 0.6 fusion.66
  49.2 0.8 fusion.67
  50.0 0.1 compare_and_fusion.3
  50.1 0.6 fusion.66
  50.8 0.8 fusion.67
  51.6 0.1 compare_and_fusion.3
  51.7 0.6 fusion.66
  52.3 0.8 fusion.67
  53.1 0.1 compare_and_fusion.3
  53.2 0.6 fusion.66
  53.9 0.8 fusion.67
  54.7 0.2 copy.35
  54.9 1.2 gather_fusion
  56.1 0.2 gather.7
  56.3 0.1 compare_and_fusion.1
  56.4 0.1 copy.30
  56.5 1.4 broadcast_select_fusion
  57.9 6.8 %all-to-all-start = ((bf16[128,2,1024]{2,1,0:T(2,128)(2,1)}), bf16[128,2,1024]{2,1,0:T(2,128)(2,1)S(1)}, u32[]{:S(2)}, u32[]{:S(2)}) async-start(bf16[128,2,1024]{2,1,0:T(2,128)(2,1)} %broadcast_select_fusion), calls=%async_computation | async-start | bytes 1048576 | tf_op jit(solution)/shard_map/all_to_all | solution.py:59
  64.7 0.1 copy.29
  64.8 0.1 add.136
  65.0 0.1 copy.28
  65.1 0.2 lt.81
  65.3 22.5 %all-to-all-done = bf16[128,2,1024]{2,1,0:T(2,128)(2,1)S(1)} async-done(((bf16[128,2,1024]{2,1,0:T(2,128)(2,1)}), bf16[128,2,1024]{2,1,0:T(2,128)(2,1)S(1)}, u32[]{:S(2)}, u32[]{:S(2)}) %all-to-all-start) | async-done | bytes 524320 | tf_op jit(solution)/shard_map/all_to_all | solution.py:59
  87.8 0.2 reshape.243
  88.0 1.8 %scatter_custom_fusion = bf16[192,1024]{1,0:T(8,128)(2,1)S(1)} fusion(s32[256]{0:T(256)S(1)} %bitcast.81, bf16[256,1024]{1,0:T(8,128)(2,1)S(1)} %reshape.243, bf16[]{:T(256)} %constant.76.clone.1), kind=kCustom, calls=%fused_computation.32 | custom fusion | bytes 393218 | tf_op jit(solution)/shard_map/scatter | solution.py:66
  89.7 18.4 %all-gather.2.cloned.1.call-done = bf16[1024,4096]{0,1:T(8,128)(2,1)} async-done(((bf16[1024,32]{0,1:T(8,128)(2,1)}), bf16[1024,4096]{0,1:T(8,128)(2,1)}) %all-gather.2.cloned.1.call-update) | async-done | bytes 8388624 | tf_op jit(solution)/shard_map/all_gather | solution.py:71
  108.1 6.3 %convolution_convert_fusion.1 = bf16[192,4096]{1,0:T(8,128)(2,1)S(1)} fusion(bf16[192,1024]{1,0:T(8,128)(2,1)S(1)} %scatter_custom_fusion, bf16[1024,4096]{0,1:T(8,128)(2,1)} %all-gather.2.cloned.1.call-done), kind=kOutput, calls=%fused_computation.28 | convolution fusion | flops 1611399168 | bytes 10354688 | tf_op jit(solution)/shard_map/dot_general | solution.py:69
  114.4 0.1 copy.40
  114.5 0.0 copy-start
  114.6 23.8 %all_to_all.10 = bf16[4,192,1024]{2,1,0:T(8,128)(2,1)S(1)} all-to-all(bf16[4,192,1024]{2,1,0:T(8,128)(2,1)S(1)} %bitcast.73), channel_id=1, replica_groups=mesh['pairs'=128,'tensor'=4] {'tensor'}, dimensions={0} | all-to-all | bytes 3145728 | tf_op jit(solution)/shard_map/all_to_all | solution.py:80
  138.3 0.3 reduce_sum.41
  138.7 0.0 copy-done
  138.7 0.9 add_convert_fusion
  (10 shorter events, 0.1 us)
Async XLA Ops:
  6.5 41.9 %copy-start.1 = (s32[256]{0:T(256)S(1)}, s32[256]{0:T(256)}, u32[]{:S(2)}) copy-start(s32[256]{0:T(256)} %param.11) | copy-start | bytes 3076
  6.5 101.6 %all-gather.2.cloned.1.call-start = ((), (), s32[]{:S(2)}) async-start(), calls=%async_computation.2 | async-start | bytes 8454144 | tf_op jit(solution)/shard_map/all_gather | solution.py:71
  57.9 29.8 %all-to-all-start = ((bf16[128,2,1024]{2,1,0:T(2,128)(2,1)}), bf16[128,2,1024]{2,1,0:T(2,128)(2,1)S(1)}, u32[]{:S(2)}, u32[]{:S(2)}) async-start(bf16[128,2,1024]{2,1,0:T(2,128)(2,1)} %broadcast_select_fusion), calls=%async_computation | async-start | bytes 1048576 | tf_op jit(solution)/shard_map/all_to_all | solution.py:59
  114.5 24.1 %copy-start = (bf16[192,1024]{1,0:T(8,128)(2,1)S(1)}, bf16[192,1024]{1,0:T(8,128)(2,1)}, u32[]{:S(2)}) copy-start(bf16[192,1024]{1,0:T(8,128)(2,1)} %param.13) | copy-start | bytes 1179652
Sparse Core Ops, SparseCore 0:
  10.5 97.5 all-gather.1

commit v5 on v2

--- a/solution.py
+++ b/solution.py
@@ -66,15 +66,41 @@
     moved_rows = landed.at[incoming_slots.reshape(-1)].set(
         incoming.reshape(-1, local_width), mode="drop"
     )
-    partial_value = jnp.dot(
-        moved_rows,
-        lax.all_gather(out_weight, "pairs", axis=1, tiled=True),
-        preferred_element_type=jnp.float32,
-    )
-    payload = lax.psum_scatter(
-        partial_value.astype(jnp.bfloat16), "tensor", scatter_dimension=1, tiled=True
-    )
-    return (residual.astype(jnp.float32) + payload.astype(jnp.float32)).astype(jnp.bfloat16)
+    tensor_parts = lax.axis_size("tensor")
+    group_width = out_weight.shape[1] // tensor_parts
+    feature_stripes = devices // tensor_parts
+    tensor_place = lax.axis_index("tensor")
+    pieces = out_weight.reshape(local_width, tensor_parts, group_width)
+    dealt = []
+    for turn in range(tensor_parts):
+        pairing = []
+        for stripe_owner in range(devices):
+            for block in range(tensor_parts):
+                piece = (block + turn) % tensor_parts
+                target = tensor_parts * (stripe_owner % feature_stripes) + piece
+                pairing.append(
+                    (stripe_owner * tensor_parts + block,
+                     target * tensor_parts + stripe_owner // feature_stripes)
+                )
+        sent = jnp.take(pieces, (tensor_place + turn) % tensor_parts, axis=1)
+        dealt.append(lax.ppermute(sent, ("pairs", "tensor"), pairing))
+    piece_here = me % tensor_parts
+    order = (piece_here - jnp.arange(tensor_parts, dtype=jnp.int32)) % tensor_parts
+    own_columns = jnp.take(jnp.stack(dealt), order, axis=0).reshape(-1, group_width)
+    group_weight_t = lax.all_gather(own_columns.T, "pairs", axis=0, tiled=True)
+    spread = jnp.broadcast_to(moved_rows[None], (tensor_parts,) + moved_rows.shape)
+    all_groups = lax.all_to_all(spread, "tensor", 0, 0, tiled=True)
+    projected = jnp.zeros(moved_rows.shape, jnp.float32)
+    for group in range(tensor_parts):
+        partial_value = lax.dot_general(
+            all_groups[group],
+            group_weight_t[:, group * local_width:(group + 1) * local_width],
+            (((1,), (1,)), ((), ())),
+            preferred_element_type=jnp.float32,
+        )
+        projected = projected + partial_value.astype(jnp.bfloat16).astype(jnp.float32)
+    projected = projected.astype(jnp.bfloat16)
+    return (residual.astype(jnp.float32) + projected.astype(jnp.float32)).astype(jnp.bfloat16)
 
 
 def solution(mesh):

time: 156 us -> 161 us (1.032)
  waiting for transfers between devices: 68.2 us -> 26.9 us
  starting transfers between devices: 6.83 us -> 35.4 us
  blocking collectives: 31.6 us -> 51.9 us
  other arithmetic: 9.73 us -> 5.85 us
  matrix products: 13.2 us -> 16.3 us
  local copies, waits for them, and re-layouts: 10.9 us -> 8.61 us
    reduce_scatter x1 -> x0, waiting for transfers between devices: 27.2 us -> none  [shards(): lax.psum_scatter(partial_value.astype(jnp.bfloat16), 'tensor', scatter_di...]
    ppermute x0 -> x4, starting transfers between devices: none -> 21.8 us  [shards(): dealt.append(lax.ppermute(sent, ('pairs', 'tensor'), pairing))]
    all_to_all x0 -> x1, blocking collectives: none -> 21.2 us  [shards(): all_groups = lax.all_to_all(spread, 'tensor', 0, 0, tiled=True)]
    all_gather x1, waiting for transfers between devices: 16.4 us -> 0.01 us  [shards(): group_weight_t = lax.all_gather(own_columns.T, 'pairs', axis=0, tiled=True)]
    all_to_all x1, starting transfers between devices: 6.78 us -> 13.6 us  [shards(): lax.all_to_all(outgoing, 'pairs', split_axis=0, concat_axis=0, tiled=True)]
    ppermute x0 -> x4, waiting for transfers between devices: none -> 3.81 us  [shards(): dealt.append(lax.ppermute(sent, ('pairs', 'tensor'), pairing))]
    dot_general x1 -> x4, matrix products: 7.53 us -> 10.6 us  [shards(): lax.dot_general(all_groups[group], group_weight_t[:, group * local_width:...]
    unnamed x8 -> x18, local copies, waits for them, and re-layouts: 6.33 us -> 3.3 us
  transfers between devices with their start and end apart: 3 -> 6, of which waited for: 3 -> 2; matrix products, arithmetic and copies ran while one was open for 16% -> 11% of each run, Pallas kernels for 0% -> 0%
where the time goes in v5:
time: 161 us; the launch traced here: 159 us
  blocking collectives  51.9 us (32%)
  starting transfers between devices  35.4 us (22%)
  waiting for transfers between devices  26.9 us (17%)
  matrix products  16.3 us (10%)
  between operations  13.7 us (9%)
  local copies, waits for them, and re-layouts  8.61 us (5%)
  other arithmetic  5.85 us (4%)
    unnamed x1, blocking collectives  30.7 us
    all_to_all x1, waiting for transfers between devices, shards(): lax.all_to_all(outgoing, 'pairs', split_axis=0, concat_axis=0, tiled=True)  23.1 us
    ppermute x4, starting transfers between devices, shards(): dealt.append(lax.ppermute(sent, ('pairs', 'tensor'), pairing))  21.8 us
    all_to_all x1, blocking collectives, shards(): all_groups = lax.all_to_all(spread, 'tensor', 0, 0, tiled=True)  21.2 us
    all_to_all x1, starting transfers between devices, shards(): lax.all_to_all(outgoing, 'pairs', split_axis=0, concat_axis=0, tiled=True)  13.6 us
    dot_general x4, matrix products, shards(): lax.dot_general(all_groups[group], group_weight_t[:, group * local_width:...  10.6 us
    ppermute x4, waiting for transfers between devices, shards(): dealt.append(lax.ppermute(sent, ('pairs', 'tensor'), pairing))  3.81 us
    unnamed x18, local copies, waits for them, and re-layouts  3.3 us
  transfers between devices with their start and end apart: 6, of which 2 were waited for; matrix products, arithmetic and copies ran while one was open for 11% of the time, Pallas kernels for 0%

profile of v5, /device:TPU:6, one launch (start us, length us, event | category | flops | bytes accessed | tf_op | source)
XLA Modules:
  0.0 158.7 jit_solution(6104164868354194815)
XLA Ops:
  6.5 0.9 select_bitcast_fusion.4
  7.4 3.6 %collective-permute-start = (bf16[1024,8]{0,1:T(8,128)(2,1)S(1)}, bf16[1024,8]{0,1:T(8,128)(2,1)S(1)}, u32[]{:S(2)}, u32[]{:S(2)}) collective-permute-start(bf16[1024,8]{0,1:T(8,128)(2,1)S(1)} %get-tuple-element.86), channel_id=1, source_target_pairs={{0,0},{1,4},{2,8},{3,12},{4,16},{5,20},{6,24},{7,28},{8,32},{9,36}... | collective-permute-start | bytes 49160 | tf_op jit(solution)/shard_map/ppermute | solution.py:86
  11.1 9.7 %collective-permute-start.3 = (bf16[1024,8]{0,1:T(8,128)(2,1)S(1)}, bf16[1024,8]{0,1:T(8,128)(2,1)S(1)}, u32[]{:S(2)}, u32[]{:S(2)}) collective-permute-start(bf16[1024,8]{0,1:T(8,128)(2,1)S(1)} %get-tuple-element.87), channel_id=1, source_target_pairs={{0,12},{1,0},{2,4},{3,8},{4,28},{5,16},{6,20},{7,24},{8,44},{9,32}... | collective-permute-start | bytes 49160 | tf_op jit(solution)/shard_map/ppermute | solution.py:86
  20.7 4.7 %collective-permute-start.2 = (bf16[1024,8]{0,1:T(8,128)(2,1)S(1)}, bf16[1024,8]{0,1:T(8,128)(2,1)S(1)}, u32[]{:S(2)}, u32[]{:S(2)}) collective-permute-start(bf16[1024,8]{0,1:T(8,128)(2,1)S(1)} %get-tuple-element.88), channel_id=1, source_target_pairs={{0,8},{1,12},{2,0},{3,4},{4,24},{5,28},{6,16},{7,20},{8,40},{9,44}... | collective-permute-start | bytes 49160 | tf_op jit(solution)/shard_map/ppermute | solution.py:86
  25.5 3.8 %collective-permute-start.1 = (bf16[1024,8]{0,1:T(8,128)(2,1)S(1)}, bf16[1024,8]{0,1:T(8,128)(2,1)S(1)}, u32[]{:S(2)}, u32[]{:S(2)}) collective-permute-start(bf16[1024,8]{0,1:T(8,128)(2,1)S(1)} %get-tuple-element.89), channel_id=1, source_target_pairs={{0,4},{1,8},{2,12},{3,0},{4,20},{5,24},{6,28},{7,16},{8,36},{9,40}... | collective-permute-start | bytes 49160 | tf_op jit(solution)/shard_map/ppermute | solution.py:86
  29.3 0.1 broadcast_bitcast_fusion
  29.4 0.0 collective-permute-done
  29.4 0.0 collective-permute-done.3
  29.4 0.0 collective-permute-done.2
  29.4 3.8 %collective-permute-done.1 = bf16[1024,8]{0,1:T(8,128)(2,1)S(1)} collective-permute-done((bf16[1024,8]{0,1:T(8,128)(2,1)S(1)}, bf16[1024,8]{0,1:T(8,128)(2,1)S(1)}, u32[]{:S(2)}, u32[]{:S(2)}) %collective-permute-start.1) | collective-permute-done | bytes 16416 | tf_op jit(solution)/shard_map/ppermute | solution.py:86
  33.2 0.0 copy-start.2
  33.2 0.6 gather_fusion.1
  33.8 0.7 select_bitcast_fusion
  34.5 0.0 all-gather.2.cloned.1.call-update
  34.5 1.3 dynamic-slice.7
  35.8 0.6 convert_reduce_fusion
  36.4 1.3 dynamic-update-slice.1
  37.7 30.7 %all-reduce = s32[128]{0:T(128)S(1)} all-reduce(s32[128]{0:T(128)S(1)} %dynamic-update-slice.1), channel_id=1, replica_groups=mesh['pairs'=128,'tensor'=4] {'pairs'}, use_global_device_ids=true, to_apply=%add | all-reduce | flops 128 | bytes 1024
  68.5 0.1 copy.20
  68.6 0.2 reduce-window.9
  68.7 0.1 reduce
  68.9 0.6 and_select_fusion.4
  69.5 0.6 and_select_fusion.3
  70.1 0.1 compare_and_fusion.2
  70.2 0.1 copy.23
  70.4 0.1 broadcast_add_fusion
  70.4 0.1 copy.27
  70.5 0.1 add.212
  70.7 0.0 copy-done
  70.7 0.2 copy.25
  70.9 0.2 copy.26
  71.1 0.2 copy.24
  71.3 6.2 %while.12 = (s32[]{:T(128)}, bf16[4,256,4,64]{1,3,2,0:T(8,128)(2,1)S(1)}, bf16[4,256,4,64]{1,3,2,0:T(8,128)(2,1)S(1)}, bf16[4,256,4,64]{1,3,2,0:T(8,128)(2,1)S(1...) while((s32[]{:T(128)}, ...), condition=%wide.region_6.7_spmd.clone, body=%wide.region_3.6_spmd.clone.sunk | while | flops 103221760 | bytes 1134941 | solution.py:44
  71.4 0.1 compare_and_fusion.4
  71.5 0.6 fusion.120
  72.1 0.8 fusion.121
  72.9 0.1 compare_and_fusion.4
  73.0 0.6 fusion.120
  73.6 0.8 fusion.121
  74.5 0.1 compare_and_fusion.4
  74.6 0.6 fusion.120
  75.2 0.8 fusion.121
  76.0 0.1 compare_and_fusion.4
  76.1 0.6 fusion.120
  76.7 0.8 fusion.121
  77.5 0.2 copy.28
  77.8 1.2 gather_fusion
  79.0 0.2 gather.16
  79.2 1.4 broadcast_select_fusion
  80.6 13.6 %all-to-all-start = ((bf16[128,2,1024]{2,1,0:T(2,128)(2,1)}), bf16[128,2,1024]{2,1,0:T(2,128)(2,1)S(1)}, u32[]{:S(2)}, u32[]{:S(2)}) async-start(bf16[128,2,1024]{2,1,0:T(2,128)(2,1)} %broadcast_select_fusion), calls=%async_computation | async-start | bytes 1048576 | tf_op jit(solution)/shard_map/all_to_all | solution.py:59
  94.2 0.1 copy.21
  94.4 0.1 lt.129
  94.5 0.1 copy.22
  94.6 0.1 add.205
  94.8 23.1 %all-to-all-done = bf16[128,2,1024]{2,1,0:T(2,128)(2,1)S(1)} async-done(((bf16[128,2,1024]{2,1,0:T(2,128)(2,1)}), bf16[128,2,1024]{2,1,0:T(2,128)(2,1)S(1)}, u32[]{:S(2)}, u32[]{:S(2)}) %all-to-all-start) | async-done | bytes 524320 | tf_op jit(solution)/shard_map/all_to_all | solution.py:59
  117.9 0.2 reshape.401
  118.1 1.8 %scatter_custom_fusion = bf16[192,1024]{1,0:T(8,128)(2,1)S(1)} fusion(s32[256]{0:T(256)S(1)} %bitcast.113, bf16[256,1024]{1,0:T(8,128)(2,1)S(1)} %reshape.401, bf16[]{:T(256)} %constant.138.clone.1), kind=kCustom, calls=%fused_computation.57 | custom fusion | bytes 393218 | tf_op jit(solution)/shard_map/scatter | solution.py:66
  119.8 0.2 broadcast_in_dim.92
  120.0 21.2 %all_to_all.10 = bf16[4,192,1024]{2,1,0:T(8,128)(2,1)S(1)} all-to-all(bf16[4,192,1024]{2,1,0:T(8,128)(2,1)S(1)} %broadcast_in_dim.92), channel_id=1, replica_groups=mesh['pairs'=128,'tensor'=4] {'tensor'}, dimensions={0} | all-to-all | bytes 3145728 | tf_op jit(solution)/shard_map/all_to_all | solution.py:92
  141.2 2.4 %fusion.83 = f32[192,1024]{1,0:T(8,128)S(1)} fusion(bf16[1024,4096]{1,0:T(8,128)(2,1)} %all-gather.2.cloned.1.call-done, bf16[4,192,1024]{2,1,0:T(8,128)(2,1)S(1)} %all_to_all.10), kind=kOutput, calls=%fused_computation.48 | convolution fusion | flops 403046400 | bytes 3276800 | tf_op jit(solution)/shard_map/dot_general | solution.py:95
  143.7 2.4 %fusion.77 = f32[192,1024]{1,0:T(8,128)S(1)} fusion(bf16[1024,4096]{1,0:T(8,128)(2,1)} %all-gather.2.cloned.1.call-done, bf16[4,192,1024]{2,1,0:T(8,128)(2,1)S(1)} %all_to_all.10), kind=kOutput, calls=%fused_computation.46 | convolution fusion | flops 403046400 | bytes 3276800 | tf_op jit(solution)/shard_map/dot_general | solution.py:95
  146.1 0.0 copy-start.3
  146.1 2.5 %fusion.71 = f32[192,1024]{1,0:T(8,128)S(1)} fusion(bf16[1024,4096]{1,0:T(8,128)(2,1)} %all-gather.2.cloned.1.call-done, bf16[4,192,1024]{2,1,0:T(8,128)(2,1)S(1)} %all_to_all.10), kind=kOutput, calls=%fused_computation.44 | convolution fusion | flops 403046400 | bytes 3276800 | tf_op jit(solution)/shard_map/dot_general | solution.py:95
  148.6 3.3 %fusion.92 = bf16[192,1024]{1,0:T(8,128)(2,1)} fusion(f32[192,1024]{1,0:T(8,128)S(1)} %fusion.83, f32[192,1024]{1,0:T(8,128)S(1)} %fusion.77, f32[192,1024]{1,0:T(8,128)S(1)} %fusion.71, bf16[1024,4096]{1,0:T(8,128)(2,1)} %all-gather.2.cloned.1.call-done, bf16[192,1024]{1,0:T(8,128)(2,1)S(1)} %copy-done.3, bf16[4,192,1024]{2,1,0:T(8,128)(2,1)S(1)} %all_to_all.10), kind=kOutput, calls=%fused_computation.51 | convolution fusion | flops 404619264 | bytes 5636096 | tf_op jit(solution)/shard_map/dot_general | solution.py:95
  (24 shorter events, 0.1 us)
Async XLA Ops:
  6.5 29.2 %copy-start.4 = (s32[256]{0:T(256)S(1)}, s32[256]{0:T(256)}, u32[]{:S(2)}) copy-start(s32[256]{0:T(256)} %param.13) | copy-start | bytes 3076
  6.5 64.2 %copy-start = (bf16[256,1024]{1,0:T(8,128)(2,1)S(1)}, bf16[256,1024]{1,0:T(8,128)(2,1)}, u32[]{:S(2)}) copy-start(bf16[256,1024]{1,0:T(8,128)(2,1)} %param.10) | copy-start | bytes 1572868
  6.5 134.7 %all-gather.2.cloned.1.call-start = ((), (), s32[]{:S(2)}) async-start(), calls=%async_computation.2 | async-start | bytes 8454144 | tf_op jit(solution)/shard_map/all_gather | solution.py:90
  6.5 64.4 %copy-start.1 = (bf16[256,1024]{1,0:T(8,128)(2,1)S(1)}, bf16[256,1024]{1,0:T(8,128)(2,1)}, u32[]{:S(2)}) copy-start(bf16[256,1024]{1,0:T(8,128)(2,1)} %param.11) | copy-start | bytes 1572868
  7.4 22.0 %collective-permute-start = (bf16[1024,8]{0,1:T(8,128)(2,1)S(1)}, bf16[1024,8]{0,1:T(8,128)(2,1)S(1)}, u32[]{:S(2)}, u32[]{:S(2)}) collective-permute-start(bf16[1024,8]{0,1:T(8,128)(2,1)S(1)} %get-tuple-element.86), channel_id=1, source_target_pairs={{0,0},{1,4},{2,8},{3,12},{4,16},{5,20},{6,24},{7,28},{8,32},{9,36}... | collective-permute-start | bytes 49160 | tf_op jit(solution)/shard_map/ppermute | solution.py:86
  11.1 18.4 %collective-permute-start.3 = (bf16[1024,8]{0,1:T(8,128)(2,1)S(1)}, bf16[1024,8]{0,1:T(8,128)(2,1)S(1)}, u32[]{:S(2)}, u32[]{:S(2)}) collective-permute-start(bf16[1024,8]{0,1:T(8,128)(2,1)S(1)} %get-tuple-element.87), channel_id=1, source_target_pairs={{0,12},{1,0},{2,4},{3,8},{4,28},{5,16},{6,20},{7,24},{8,44},{9,32}... | collective-permute-start | bytes 49160 | tf_op jit(solution)/shard_map/ppermute | solution.py:86
  20.7 8.7 %collective-permute-start.2 = (bf16[1024,8]{0,1:T(8,128)(2,1)S(1)}, bf16[1024,8]{0,1:T(8,128)(2,1)S(1)}, u32[]{:S(2)}, u32[]{:S(2)}) collective-permute-start(bf16[1024,8]{0,1:T(8,128)(2,1)S(1)} %get-tuple-element.88), channel_id=1, source_target_pairs={{0,8},{1,12},{2,0},{3,4},{4,24},{5,28},{6,16},{7,20},{8,40},{9,44}... | collective-permute-start | bytes 49160 | tf_op jit(solution)/shard_map/ppermute | solution.py:86
  25.5 7.7 %collective-permute-start.1 = (bf16[1024,8]{0,1:T(8,128)(2,1)S(1)}, bf16[1024,8]{0,1:T(8,128)(2,1)S(1)}, u32[]{:S(2)}, u32[]{:S(2)}) collective-permute-start(bf16[1024,8]{0,1:T(8,128)(2,1)S(1)} %get-tuple-element.89), channel_id=1, source_target_pairs={{0,4},{1,8},{2,12},{3,0},{4,20},{5,24},{6,28},{7,16},{8,36},{9,40}... | collective-permute-start | bytes 49160 | tf_op jit(solution)/shard_map/ppermute | solution.py:86
  33.2 37.9 %copy-start.2 = (bf16[256,1024]{1,0:T(8,128)(2,1)S(1)}, bf16[256,1024]{1,0:T(8,128)(2,1)}, u32[]{:S(2)}) copy-start(bf16[256,1024]{1,0:T(8,128)(2,1)} %param.12) | copy-start | bytes 1572868
  80.6 37.3 %all-to-all-start = ((bf16[128,2,1024]{2,1,0:T(2,128)(2,1)}), bf16[128,2,1024]{2,1,0:T(2,128)(2,1)S(1)}, u32[]{:S(2)}, u32[]{:S(2)}) async-start(bf16[128,2,1024]{2,1,0:T(2,128)(2,1)} %broadcast_select_fusion), calls=%async_computation | async-start | bytes 1048576 | tf_op jit(solution)/shard_map/all_to_all | solution.py:59
  146.1 2.5 %copy-start.3 = (bf16[192,1024]{1,0:T(8,128)(2,1)S(1)}, bf16[192,1024]{1,0:T(8,128)(2,1)}, u32[]{:S(2)}) copy-start(bf16[192,1024]{1,0:T(8,128)(2,1)} %param.15) | copy-start | bytes 1179652
Sparse Core Ops, SparseCore 0:
  34.6 102.6 all-gather.1

commit v6 on v2

--- a/solution.py
+++ b/solution.py
@@ -66,15 +66,24 @@
     moved_rows = landed.at[incoming_slots.reshape(-1)].set(
         incoming.reshape(-1, local_width), mode="drop"
     )
-    partial_value = jnp.dot(
-        moved_rows,
-        lax.all_gather(out_weight, "pairs", axis=1, tiled=True),
-        preferred_element_type=jnp.float32,
-    )
-    payload = lax.psum_scatter(
-        partial_value.astype(jnp.bfloat16), "tensor", scatter_dimension=1, tiled=True
-    )
-    return (residual.astype(jnp.float32) + payload.astype(jnp.float32)).astype(jnp.bfloat16)
+    group_weight = lax.all_gather(out_weight, "pairs", axis=1, tiled=True)
+    tensor_parts = lax.axis_size("tensor")
+    tensor_place = lax.axis_index("tensor")
+
+    def group_product(group):
+        columns = lax.dynamic_slice_in_dim(group_weight, group * local_width, local_width, 1)
+        return jnp.dot(moved_rows, columns, preferred_element_type=jnp.float32).astype(jnp.bfloat16)
+
+    arrived = []
+    for shift in range(1, tensor_parts):
+        sent = group_product((tensor_place + shift) % tensor_parts)
+        pairing = [(i, (i + shift) % tensor_parts) for i in range(tensor_parts)]
+        arrived.append(lax.ppermute(sent, "tensor", pairing))
+    total = group_product(tensor_place).astype(jnp.float32)
+    for part in arrived:
+        total = total + part.astype(jnp.float32)
+    projected = total.astype(jnp.bfloat16)
+    return (residual.astype(jnp.float32) + projected.astype(jnp.float32)).astype(jnp.bfloat16)
 
 
 def solution(mesh):

time: 156 us -> 153 us (0.981)
  waiting for transfers between devices: 68.2 us -> 55 us
  starting transfers between devices: 6.83 us -> 15.4 us
  matrix products: 13.2 us -> 16.2 us
  other arithmetic: 9.73 us -> 7.97 us
    reduce_scatter x1 -> x0, waiting for transfers between devices: 27.2 us -> none  [shards(): lax.psum_scatter(partial_value.astype(jnp.bfloat16), 'tensor', scatter_di...]
    ppermute x0 -> x3, waiting for transfers between devices: none -> 14.1 us  [shards(): arrived.append(lax.ppermute(sent, 'tensor', pairing))]
    ppermute x0 -> x3, starting transfers between devices: none -> 8.64 us  [shards(): arrived.append(lax.ppermute(sent, 'tensor', pairing))]
    dot_general x1 -> x4, matrix products: 7.53 us -> 10.6 us  [group_product(): jnp.dot(moved_rows, columns, preferred_element_type=jnp.float32)]
    convert_element_type x1 -> x0, other arithmetic: 1.88 us -> none  [shards(): (residual.astype(jnp.float32) + payload.astype(jnp.float32)).astype(jnp.b...]
  transfers between devices with their start and end apart: 3 -> 5, of which waited for: 3 -> 5; matrix products, arithmetic and copies ran while one was open for 16% -> 20% of each run, Pallas kernels for 0% -> 0%
where the time goes in v6:
time: 153 us; the launch traced here: 151 us
  waiting for transfers between devices  55 us (36%)
  blocking collectives  31.6 us (21%)
  matrix products  16.2 us (11%)
  starting transfers between devices  15.4 us (10%)
  between operations  13.6 us (9%)
  local copies, waits for them, and re-layouts  11 us (7%)
  other arithmetic  7.97 us (5%)
    unnamed x1, blocking collectives  31.6 us
    all_to_all x1, waiting for transfers between devices, shards(): lax.all_to_all(outgoing, 'pairs', split_axis=0, concat_axis=0, tiled=True)  23.9 us
    all_gather x1, waiting for transfers between devices, shards(): group_weight = lax.all_gather(out_weight, 'pairs', axis=1, tiled=True)  16.4 us
    ppermute x3, waiting for transfers between devices, shards(): arrived.append(lax.ppermute(sent, 'tensor', pairing))  14.1 us
    dot_general x4, matrix products, group_product(): jnp.dot(moved_rows, columns, preferred_element_type=jnp.float32)  10.6 us
    ppermute x3, starting transfers between devices, shards(): arrived.append(lax.ppermute(sent, 'tensor', pairing))  8.64 us
    all_to_all x1, starting transfers between devices, shards(): lax.all_to_all(outgoing, 'pairs', split_axis=0, concat_axis=0, tiled=True)  6.76 us
    unnamed x8, local copies, waits for them, and re-layouts  6.41 us
  transfers between devices with their start and end apart: 5, of which 5 were waited for; matrix products, arithmetic and copies ran while one was open for 20% of the time, Pallas kernels for 0%

profile of v6, /device:TPU:6, one launch (start us, length us, event | category | flops | bytes accessed | tf_op | source)
XLA Modules:
  0.0 151.0 jit_solution(14459260997960229809)
XLA Ops:
  6.5 0.0 all-gather.2.cloned.1.call-start
  6.5 0.7 all-gather.2.cloned.1.call-update
  7.3 1.3 dynamic-slice
  8.6 1.3 convert_reduce_fusion
  9.9 1.4 dynamic-update-slice
  11.3 31.6 %all-reduce = s32[128]{0:T(128)S(1)} all-reduce(s32[128]{0:T(128)S(1)} %dynamic-update-slice), channel_id=1, replica_groups=mesh['pairs'=128,'tensor'=4] {'pairs'}, use_global_device_ids=true, to_apply=%add | all-reduce | flops 128 | bytes 1024
  42.9 0.1 copy.20
  43.0 0.2 reduce-window.9
  43.2 0.1 reduce
  43.3 0.6 and_select_fusion.2
  43.9 0.7 and_select_fusion.1
  44.6 0.1 broadcast_add_fusion
  44.6 0.1 copy.27
  44.8 0.1 add.183
  44.9 1.2 copy.24
  46.2 1.2 copy.25
  47.4 1.2 copy.26
  48.7 9.2 %while.11 = (s32[]{:T(128)}, bf16[4,256,4,64]{1,3,2,0:T(8,128)(2,1)S(1)}, bf16[4,256,4,64]{1,3,2,0:T(8,128)(2,1)S(1)}, bf16[4,256,4,64]{1,3,2,0:T(8,128)(2,1)S(1...) while((s32[]{:T(128)}, ...), condition=%wide.region_6.7_spmd.clone, body=%wide.region_3.6_spmd.clone.sunk | while | flops 103221760 | bytes 1134933 | solution.py:44
  48.7 0.9 compare_and_fusion.3
  49.5 0.6 fusion.97
  50.2 0.8 fusion.98
  51.0 0.9 compare_and_fusion.3
  51.8 0.6 fusion.97
  52.5 0.8 fusion.98
  53.3 0.9 compare_and_fusion.3
  54.1 0.6 fusion.97
  54.8 0.8 fusion.98
  55.6 0.9 compare_and_fusion.3
  56.4 0.6 fusion.97
  57.1 0.8 fusion.98
  57.9 0.2 copy.28
  58.1 0.0 copy-start
  58.1 1.2 gather_fusion
  59.3 0.2 gather.7
  59.5 0.1 compare_and_fusion.1
  59.6 0.1 copy.23
  59.7 1.4 broadcast_select_fusion
  61.1 6.8 %all-to-all-start = ((bf16[128,2,1024]{2,1,0:T(2,128)(2,1)}), bf16[128,2,1024]{2,1,0:T(2,128)(2,1)S(1)}, u32[]{:S(2)}, u32[]{:S(2)}) async-start(bf16[128,2,1024]{2,1,0:T(2,128)(2,1)} %broadcast_select_fusion), calls=%async_computation | async-start | bytes 1048576 | tf_op jit(solution)/shard_map/all_to_all | solution.py:59
  68.0 0.1 copy.22
  68.1 0.1 add.176
  68.2 0.1 copy.21
  68.4 0.2 lt.107
  68.5 23.9 %all-to-all-done = bf16[128,2,1024]{2,1,0:T(2,128)(2,1)S(1)} async-done(((bf16[128,2,1024]{2,1,0:T(2,128)(2,1)}), bf16[128,2,1024]{2,1,0:T(2,128)(2,1)S(1)}, u32[]{:S(2)}, u32[]{:S(2)}) %all-to-all-start) | async-done | bytes 524320 | tf_op jit(solution)/shard_map/all_to_all | solution.py:59
  92.4 0.2 reshape.239
  92.6 1.8 %scatter_custom_fusion = bf16[192,1024]{1,0:T(8,128)(2,1)S(1)} fusion(s32[256]{0:T(256)S(1)} %bitcast.74, bf16[256,1024]{1,0:T(8,128)(2,1)S(1)} %reshape.239, bf16[]{:T(256)} %constant.99.clone.1), kind=kCustom, calls=%fused_computation.44 | custom fusion | bytes 393218 | tf_op jit(solution)/shard_map/scatter | solution.py:66
  94.4 16.4 %all-gather.2.cloned.1.call-done = bf16[1024,4096]{0,1:T(8,128)(2,1)} async-done(((bf16[1024,32]{0,1:T(8,128)(2,1)}), bf16[1024,4096]{0,1:T(8,128)(2,1)}) %all-gather.2.cloned.1.call-update) | async-done | bytes 8388624 | tf_op jit(solution)/shard_map/all_gather | solution.py:69
  110.7 2.4 %fusion.56 = bf16[192,1024]{1,0:T(8,128)(2,1)S(1)} fusion(bf16[192,1024]{1,0:T(8,128)(2,1)S(1)} %scatter_custom_fusion, bf16[1024,4096]{0,1:T(8,128)(2,1)} %all-gather.2.cloned.1.call-done, s32[]{:T(128)S(6)} %select_n.120), kind=kOutput, calls=%fused_computation.38 | convolution fusion | flops 402849792 | bytes 2883588 | tf_op jit(solution)/shard_map/dot_general | solution.py:75
  113.2 2.4 %collective-permute-start = (bf16[192,1024]{1,0:T(8,128)(2,1)S(1)}, bf16[192,1024]{1,0:T(8,128)(2,1)S(1)}, u32[]{:S(2)}, u32[]{:S(2)}) collective-permute-start(bf16[192,1024]{1,0:T(8,128)(2,1)S(1)} %fusion.56), channel_id=1, source_target_pairs={{0,1},{1,2},{2,3},{3,0},{4,5},{5,6},{6,7},{7,4},{8,9},{9,10},{10,1... | collective-permute-start | bytes 1179656 | tf_op jit(solution)/shard_map/ppermute | solution.py:81
  115.5 2.4 %fusion.59 = bf16[192,1024]{1,0:T(8,128)(2,1)S(1)} fusion(bf16[192,1024]{1,0:T(8,128)(2,1)S(1)} %scatter_custom_fusion, bf16[1024,4096]{0,1:T(8,128)(2,1)} %all-gather.2.cloned.1.call-done, s32[]{:T(128)S(6)} %select_n.122), kind=kOutput, calls=%fused_computation.39 | convolution fusion | flops 402849792 | bytes 2883588 | tf_op jit(solution)/shard_map/dot_general | solution.py:75
  118.0 4.4 %collective-permute-start.1 = (bf16[192,1024]{1,0:T(8,128)(2,1)S(1)}, bf16[192,1024]{1,0:T(8,128)(2,1)S(1)}, u32[]{:S(2)}, u32[]{:S(2)}) collective-permute-start(bf16[192,1024]{1,0:T(8,128)(2,1)S(1)} %fusion.59), channel_id=1, source_target_pairs={{0,2},{1,3},{2,0},{3,1},{4,6},{5,7},{6,4},{7,5},{8,10},{9,11},{10,... | collective-permute-start | bytes 1179656 | tf_op jit(solution)/shard_map/ppermute | solution.py:81
  122.4 2.4 %fusion.62 = bf16[192,1024]{1,0:T(8,128)(2,1)S(1)} fusion(bf16[192,1024]{1,0:T(8,128)(2,1)S(1)} %scatter_custom_fusion, bf16[1024,4096]{0,1:T(8,128)(2,1)} %all-gather.2.cloned.1.call-done, s32[]{:T(128)S(6)} %select_n.124), kind=kOutput, calls=%fused_computation.40 | convolution fusion | flops 402849792 | bytes 2883588 | tf_op jit(solution)/shard_map/dot_general | solution.py:75
  124.8 1.9 %collective-permute-start.2 = (bf16[192,1024]{1,0:T(8,128)(2,1)S(1)}, bf16[192,1024]{1,0:T(8,128)(2,1)S(1)}, u32[]{:S(2)}, u32[]{:S(2)}) collective-permute-start(bf16[192,1024]{1,0:T(8,128)(2,1)S(1)} %fusion.62), channel_id=1, source_target_pairs={{0,3},{1,0},{2,1},{3,2},{4,7},{5,4},{6,5},{7,6},{8,11},{9,8},{10,9... | collective-permute-start | bytes 1179656 | tf_op jit(solution)/shard_map/ppermute | solution.py:81
  126.7 0.3 collective-permute-done
  127.0 6.4 %collective-permute-done.1 = bf16[192,1024]{1,0:T(8,128)(2,1)S(1)} collective-permute-done((bf16[192,1024]{1,0:T(8,128)(2,1)S(1)}, bf16[192,1024]{1,0:T(8,128)(2,1)S(1)}, u32[]{:S(2)}, u32[]{:S(2)}) %collective-permute-start.1) | collective-permute-done | bytes 393248 | tf_op jit(solution)/shard_map/ppermute | solution.py:81
  133.4 7.4 %collective-permute-done.2 = bf16[192,1024]{1,0:T(8,128)(2,1)S(1)} collective-permute-done((bf16[192,1024]{1,0:T(8,128)(2,1)S(1)}, bf16[192,1024]{1,0:T(8,128)(2,1)S(1)}, u32[]{:S(2)}, u32[]{:S(2)}) %collective-permute-start.2) | collective-permute-done | bytes 393248 | tf_op jit(solution)/shard_map/ppermute | solution.py:81
  140.8 0.0 copy-done
  140.8 3.3 %add_convert_fusion = bf16[192,1024]{1,0:T(8,128)(2,1)} fusion(bf16[192,1024]{1,0:T(8,128)(2,1)S(1)} %copy-done, bf16[192,1024]{1,0:T(8,128)(2,1)S(1)} %collective-permute-done.2, bf16[192,1024]{1,0:T(8,128)(2,1)S(1)} %collective-permute-done.1, bf16[192,1024]{1,0:T(8,128)(2,1)S(1)} %collective-permute-done, bf16[192,1024]{1,0:T(8,128)(2,1)S(1)} %scatter_custom_fusion, ...), kind=kOutput, calls=%fused_computation.42 | convolution fusion | flops 405209088 | bytes 4456452 | tf_op jit(solution)/shard_map/dot_general | solution.py:75
  (10 shorter events, 0.1 us)
Async XLA Ops:
  6.5 104.2 %all-gather.2.cloned.1.call-start = ((), (), s32[]{:S(2)}) async-start(), calls=%async_computation.1 | async-start | bytes 8454144 | tf_op jit(solution)/shard_map/all_gather | solution.py:69
  58.1 82.7 %copy-start = (bf16[192,1024]{1,0:T(8,128)(2,1)S(1)}, bf16[192,1024]{1,0:T(8,128)(2,1)}, u32[]{:S(2)}) copy-start(bf16[192,1024]{1,0:T(8,128)(2,1)} %param.13) | copy-start | bytes 1179652
  61.1 31.3 %all-to-all-start = ((bf16[128,2,1024]{2,1,0:T(2,128)(2,1)}), bf16[128,2,1024]{2,1,0:T(2,128)(2,1)S(1)}, u32[]{:S(2)}, u32[]{:S(2)}) async-start(bf16[128,2,1024]{2,1,0:T(2,128)(2,1)} %broadcast_select_fusion), calls=%async_computation | async-start | bytes 1048576 | tf_op jit(solution)/shard_map/all_to_all | solution.py:59
  113.2 13.8 %collective-permute-start = (bf16[192,1024]{1,0:T(8,128)(2,1)S(1)}, bf16[192,1024]{1,0:T(8,128)(2,1)S(1)}, u32[]{:S(2)}, u32[]{:S(2)}) collective-permute-start(bf16[192,1024]{1,0:T(8,128)(2,1)S(1)} %fusion.56), channel_id=1, source_target_pairs={{0,1},{1,2},{2,3},{3,0},{4,5},{5,6},{6,7},{7,4},{8,9},{9,10},{10,1... | collective-permute-start | bytes 1179656 | tf_op jit(solution)/shard_map/ppermute | solution.py:81
  118.0 15.4 %collective-permute-start.1 = (bf16[192,1024]{1,0:T(8,128)(2,1)S(1)}, bf16[192,1024]{1,0:T(8,128)(2,1)S(1)}, u32[]{:S(2)}, u32[]{:S(2)}) collective-permute-start(bf16[192,1024]{1,0:T(8,128)(2,1)S(1)} %fusion.59), channel_id=1, source_target_pairs={{0,2},{1,3},{2,0},{3,1},{4,6},{5,7},{6,4},{7,5},{8,10},{9,11},{10,... | collective-permute-start | bytes 1179656 | tf_op jit(solution)/shard_map/ppermute | solution.py:81
  124.8 16.0 %collective-permute-start.2 = (bf16[192,1024]{1,0:T(8,128)(2,1)S(1)}, bf16[192,1024]{1,0:T(8,128)(2,1)S(1)}, u32[]{:S(2)}, u32[]{:S(2)}) collective-permute-start(bf16[192,1024]{1,0:T(8,128)(2,1)S(1)} %fusion.62), channel_id=1, source_target_pairs={{0,3},{1,0},{2,1},{3,2},{4,7},{5,4},{6,5},{7,6},{8,11},{9,8},{10,9... | collective-permute-start | bytes 1179656 | tf_op jit(solution)/shard_map/ppermute | solution.py:81
Sparse Core Ops, SparseCore 0:
  10.5 100.2 all-gather.1

commit v7 on v2

--- a/solution.py
+++ b/solution.py
@@ -66,15 +66,24 @@
     moved_rows = landed.at[incoming_slots.reshape(-1)].set(
         incoming.reshape(-1, local_width), mode="drop"
     )
-    partial_value = jnp.dot(
-        moved_rows,
-        lax.all_gather(out_weight, "pairs", axis=1, tiled=True),
-        preferred_element_type=jnp.float32,
+    tensor_parts = lax.axis_size("tensor")
+    half = local_width // 2
+    group_weight = lax.all_gather(out_weight, "pairs", axis=1, tiled=True).reshape(
+        local_width, tensor_parts, 2, half
     )
-    payload = lax.psum_scatter(
-        partial_value.astype(jnp.bfloat16), "tensor", scatter_dimension=1, tiled=True
+    first = jnp.einsum(
+        "rk,kgn->rgn", moved_rows, group_weight[:, :, 0], preferred_element_type=jnp.float32
+    ).astype(jnp.bfloat16)
+    summed_first = lax.psum_scatter(
+        first.reshape(balanced_rows, -1), "tensor", scatter_dimension=1, tiled=True
     )
-    return (residual.astype(jnp.float32) + payload.astype(jnp.float32)).astype(jnp.bfloat16)
+    second = jnp.einsum(
+        "rk,kgn->grn", moved_rows, group_weight[:, :, 1], preferred_element_type=jnp.float32
+    ).astype(jnp.bfloat16)
+    received = lax.all_to_all(second, "tensor", 0, 0, tiled=True)
+    summed_second = jnp.sum(received.astype(jnp.float32), axis=0).astype(jnp.bfloat16)
+    projected = jnp.concatenate([summed_first, summed_second], axis=1)
+    return (residual.astype(jnp.float32) + projected.astype(jnp.float32)).astype(jnp.bfloat16)
 
 
 def solution(mesh):

time: 156 us -> 153 us (0.981)
  waiting for transfers between devices: 68.2 us -> 44.2 us
  blocking collectives: 31.6 us -> 51.8 us
    reduce_scatter x1, waiting for transfers between devices: 27.2 us -> 3.18 us  [shards(): lax.psum_scatter(first.reshape(balanced_rows, -1), 'tensor', scatter_dime...]
    all_to_all x0 -> x1, blocking collectives: none -> 20.2 us  [shards(): received = lax.all_to_all(second, 'tensor', 0, 0, tiled=True)]
    dot_general x1 -> x2, matrix products: 7.53 us -> 7.48 us  [the longest x1 3.77 us: shards(): jnp.einsum('rk,kgn->grn', moved_rows, group_weight[:, :, 1], preferred_el...]
  transfers between devices with their start and end apart: 3 -> 3, of which waited for: 3 -> 3; matrix products, arithmetic and copies ran while one was open for 16% -> 19% of each run, Pallas kernels for 0% -> 0%
where the time goes in v7:
time: 153 us; the launch traced here: 151 us
  blocking collectives  51.8 us (34%)
  waiting for transfers between devices  44.2 us (29%)
  between operations  13.5 us (9%)
  matrix products  13.1 us (9%)
  local copies, waits for them, and re-layouts  11.9 us (8%)
  other arithmetic  9.79 us (6%)
  starting transfers between devices  6.82 us (4%)
    unnamed x1, blocking collectives  31.6 us
    all_to_all x1, waiting for transfers between devices, shards(): lax.all_to_all(outgoing, 'pairs', split_axis=0, concat_axis=0, tiled=True)  23.8 us
    all_to_all x1, blocking collectives, shards(): received = lax.all_to_all(second, 'tensor', 0, 0, tiled=True)  20.2 us
    all_gather x1, waiting for transfers between devices, shards(): lax.all_gather(out_weight, 'pairs', axis=1, tiled=True)  16.4 us
    all_to_all x1, starting transfers between devices, shards(): lax.all_to_all(outgoing, 'pairs', split_axis=0, concat_axis=0, tiled=True)  6.78 us
    unnamed x8, local copies, waits for them, and re-layouts  6.33 us
    dot_general x1, matrix products, shards(): jnp.einsum('rk,kgn->grn', moved_rows, group_weight[:, :, 1], preferred_el...  3.77 us
    dot_general x1, matrix products, shards(): jnp.einsum('rk,kgn->rgn', moved_rows, group_weight[:, :, 0], preferred_el...  3.71 us
  transfers between devices with their start and end apart: 3, of which 3 were waited for; matrix products, arithmetic and copies ran while one was open for 19% of the time, Pallas kernels for 0%

profile of v7, /device:TPU:6, one launch (start us, length us, event | category | flops | bytes accessed | tf_op | source)
XLA Modules:
  0.0 151.3 jit_solution(17605546501687202835)
XLA Ops:
  6.5 0.0 all-gather.2.cloned.1.call-start
  6.5 0.7 all-gather.2.cloned.1.call-update
  7.3 1.3 dynamic-slice
  8.6 1.3 convert_reduce_fusion
  9.9 1.3 dynamic-update-slice
  11.2 31.6 %all-reduce = s32[128]{0:T(128)S(1)} all-reduce(s32[128]{0:T(128)S(1)} %dynamic-update-slice), channel_id=1, replica_groups=mesh['pairs'=128,'tensor'=4] {'pairs'}, use_global_device_ids=true, to_apply=%add | all-reduce | flops 128 | bytes 1024
  42.8 0.1 copy.23
  42.9 0.2 reduce-window.9
  43.1 0.1 reduce.1
  43.2 0.6 and_select_fusion.2
  43.8 0.6 and_select_fusion.1
  44.4 0.1 broadcast_add_fusion
  44.4 0.1 copy.30
  44.6 0.1 add.145
  44.7 1.3 copy.27
  45.9 1.2 copy.28
  47.2 1.2 copy.29
  48.4 9.2 %while.11 = (s32[]{:T(128)}, bf16[4,256,4,64]{1,3,2,0:T(8,128)(2,1)S(1)}, bf16[4,256,4,64]{1,3,2,0:T(8,128)(2,1)S(1)}, bf16[4,256,4,64]{1,3,2,0:T(8,128)(2,1)S(1...) while((s32[]{:T(128)}, ...), condition=%wide.region_6.7_spmd.clone, body=%wide.region_3.6_spmd.clone.sunk | while | flops 103221760 | bytes 1134933 | solution.py:44
  48.5 0.9 compare_and_fusion.3
  49.3 0.6 fusion.72
  50.0 0.8 fusion.73
  50.8 0.9 compare_and_fusion.3
  51.6 0.6 fusion.72
  52.3 0.8 fusion.73
  53.1 0.9 compare_and_fusion.3
  53.9 0.6 fusion.72
  54.6 0.8 fusion.73
  55.4 0.9 compare_and_fusion.3
  56.3 0.6 fusion.72
  56.9 0.8 fusion.73
  57.7 0.2 copy.31
  57.9 1.2 gather_fusion
  59.1 0.2 gather.7
  59.3 0.1 compare_and_fusion.1
  59.4 0.1 copy.26
  59.5 1.4 broadcast_select_fusion
  61.0 6.8 %all-to-all-start = ((bf16[128,2,1024]{2,1,0:T(2,128)(2,1)}), bf16[128,2,1024]{2,1,0:T(2,128)(2,1)S(1)}, u32[]{:S(2)}, u32[]{:S(2)}) async-start(bf16[128,2,1024]{2,1,0:T(2,128)(2,1)} %broadcast_select_fusion), calls=%async_computation | async-start | bytes 1048576 | tf_op jit(solution)/shard_map/all_to_all | solution.py:59
  67.7 0.0 reduce-scatter.2.cloned.1.call-start
  67.8 0.1 copy.25
  67.9 0.1 add.138
  68.0 0.1 copy.24
  68.2 0.2 lt.81
  68.4 23.8 %all-to-all-done = bf16[128,2,1024]{2,1,0:T(2,128)(2,1)S(1)} async-done(((bf16[128,2,1024]{2,1,0:T(2,128)(2,1)}), bf16[128,2,1024]{2,1,0:T(2,128)(2,1)S(1)}, u32[]{:S(2)}, u32[]{:S(2)}) %all-to-all-start) | async-done | bytes 524320 | tf_op jit(solution)/shard_map/all_to_all | solution.py:59
  92.2 0.2 reshape.247
  92.4 1.8 %scatter_custom_fusion = bf16[192,1024]{1,0:T(8,128)(2,1)S(1)} fusion(s32[256]{0:T(256)S(1)} %bitcast.98, bf16[256,1024]{1,0:T(8,128)(2,1)S(1)} %reshape.247, bf16[]{:T(256)} %constant.76.clone.1), kind=kCustom, calls=%fused_computation.40 | custom fusion | bytes 393218 | tf_op jit(solution)/shard_map/scatter | solution.py:66
  94.1 16.4 %all-gather.2.cloned.1.call-done = bf16[1024,4096]{0,1:T(8,128)(2,1)} async-done(((bf16[1024,32]{0,1:T(8,128)(2,1)}), bf16[1024,4096]{0,1:T(8,128)(2,1)}) %all-gather.2.cloned.1.call-update) | async-done | bytes 8388624 | tf_op jit(solution)/shard_map/all_gather | solution.py:71
  110.6 3.7 %fusion.47 = bf16[4,24,8,512]{3,2,1,0:T(8,128)(2,1)S(1)} fusion(bf16[1024,4,2,512]{0,3,2,1:T(8,128)(2,1)} %bitcast.99, bf16[192,1024]{1,0:T(8,128)(2,1)S(1)} %scatter_custom_fusion), kind=kOutput, calls=%fused_computation.35 | convolution fusion | flops 805699584 | bytes 5373952 | tf_op jit(solution)/shard_map/rk,kgn->rgn/dot_general | solution.py:74
  114.3 1.0 copy.38
  115.3 0.0 reduce-scatter.2.cloned.1.call-update
  115.3 0.0 copy-start
  115.4 3.8 %fusion.46 = bf16[4,192,512]{2,1,0:T(8,128)(2,1)S(1)} fusion(bf16[1024,4,2,512]{0,3,2,1:T(8,128)(2,1)} %bitcast.100, bf16[192,1024]{1,0:T(8,128)(2,1)S(1)} %scatter_custom_fusion), kind=kOutput, calls=%fused_computation.34 | convolution fusion | flops 805699584 | bytes 5373952 | tf_op jit(solution)/shard_map/rk,kgn->grn/dot_general | solution.py:80
  119.1 20.2 %all_to_all.10 = bf16[4,192,512]{2,1,0:T(8,128)(2,1)S(1)} all-to-all(bf16[4,192,512]{2,1,0:T(8,128)(2,1)S(1)} %fusion.46), channel_id=1, replica_groups=mesh['pairs'=128,'tensor'=4] {'tensor'}, dimensions={0} | all-to-all | bytes 1572864 | tf_op jit(solution)/shard_map/all_to_all | solution.py:83
  139.4 0.1 reduce_sum.41
  139.5 3.2 %reduce-scatter.2.cloned.1.call-done = bf16[192,512]{1,0:T(8,128)(2,1)} async-done(((bf16[192,2048]{1,0:T(8,128)(2,1)}), bf16[192,512]{1,0:T(8,128)(2,1)}) %reduce-scatter.2.cloned.1.call-update) | async-done | bytes 196624 | tf_op jit(solution)/shard_map/reduce_scatter | solution.py:77
  142.7 0.0 copy-done
  142.7 1.8 %add_convert_fusion = bf16[192,1024]{1,0:T(8,128)(2,1)} fusion(bf16[192,1024]{1,0:T(8,128)(2,1)S(1)} %copy-done, bf16[192,512]{1,0:T(8,128)(2,1)S(1)} %reduce_sum.41, bf16[192,512]{1,0:T(8,128)(2,1)} %reduce-scatter.2.cloned.1.call-done), kind=kLoop, calls=%fused_computation.37 | loop fusion | flops 1376256 | bytes 1179648 | tf_op jit(solution)/shard_map/convert_element_type | solution.py:86
  (10 shorter events, 0.1 us)
Async XLA Ops:
  6.5 104.0 %all-gather.2.cloned.1.call-start = ((), (), s32[]{:S(2)}) async-start(), calls=%async_computation.3 | async-start | bytes 8454144 | tf_op jit(solution)/shard_map/all_gather | solution.py:71
  61.0 31.2 %all-to-all-start = ((bf16[128,2,1024]{2,1,0:T(2,128)(2,1)}), bf16[128,2,1024]{2,1,0:T(2,128)(2,1)S(1)}, u32[]{:S(2)}, u32[]{:S(2)}) async-start(bf16[128,2,1024]{2,1,0:T(2,128)(2,1)} %broadcast_select_fusion), calls=%async_computation | async-start | bytes 1048576 | tf_op jit(solution)/shard_map/all_to_all | solution.py:59
  67.7 74.9 %reduce-scatter.2.cloned.1.call-start = ((), (), s32[]{:S(2)}) async-start(), calls=%async_computation.4 | async-start | bytes 983040 | tf_op jit(solution)/shard_map/reduce_scatter | solution.py:77
  115.3 27.3 %copy-start = (bf16[192,1024]{1,0:T(8,128)(2,1)S(1)}, bf16[192,1024]{1,0:T(8,128)(2,1)}, u32[]{:S(2)}) copy-start(bf16[192,1024]{1,0:T(8,128)(2,1)} %param.13) | copy-start | bytes 1179652
Sparse Core Ops, SparseCore 0:
  10.5 100.0 all-gather.1
  115.5 27.1 reduce-scatter.1

commit v8 on v2

--- a/solution.py
+++ b/solution.py
@@ -71,10 +71,21 @@
         lax.all_gather(out_weight, "pairs", axis=1, tiled=True),
         preferred_element_type=jnp.float32,
     )
-    payload = lax.psum_scatter(
-        partial_value.astype(jnp.bfloat16), "tensor", scatter_dimension=1, tiled=True
-    )
-    return (residual.astype(jnp.float32) + payload.astype(jnp.float32)).astype(jnp.bfloat16)
+    tensor_place = lax.axis_index("tensor")
+    groups = partial_value.astype(jnp.bfloat16).reshape(balanced_rows, 4, local_width)
+    first_partner = tensor_place + 1 - 2 * (tensor_place % 2)
+    second_partner = 3 - tensor_place
+
+    def pick(group):
+        return lax.dynamic_index_in_dim(groups, group, 1, False)
+
+    sent = jnp.stack([pick(first_partner), pick(3 - first_partner)])
+    came = lax.ppermute(sent, "tensor", [(0, 1), (1, 0), (2, 3), (3, 2)])
+    kept = jnp.stack([pick(tensor_place), pick(second_partner)])
+    pair_sums = kept.astype(jnp.float32) + came.astype(jnp.float32)
+    other_pair = lax.ppermute(pair_sums[1], "tensor", [(0, 3), (3, 0), (1, 2), (2, 1)])
+    projected = (pair_sums[0] + other_pair).astype(jnp.bfloat16)
+    return (residual.astype(jnp.float32) + projected.astype(jnp.float32)).astype(jnp.bfloat16)
 
 
 def solution(mesh):

time: 156 us -> 170 us (1.090)
  waiting for transfers between devices: 68.2 us -> 79.6 us
  starting transfers between devices: 6.83 us -> 12.3 us
  other arithmetic: 9.73 us -> 6.23 us
  local copies, waits for them, and re-layouts: 10.9 us -> 14.2 us
    ppermute x0 -> x2, waiting for transfers between devices: none -> 37.9 us  [the longest x1 19.4 us: shards(): lax.ppermute(pair_sums[1], 'tensor', [(0, 3), (3, 0), (1, 2), (2, 1)])]
    reduce_scatter x1 -> x0, waiting for transfers between devices: 27.2 us -> none  [shards(): lax.psum_scatter(partial_value.astype(jnp.bfloat16), 'tensor', scatter_di...]
    ppermute x0 -> x2, starting transfers between devices: none -> 5.52 us  [the longest x1 2.86 us: shards(): came = lax.ppermute(sent, 'tensor', [(0, 1), (1, 0), (2, 3), (3, 2)])]
    dynamic_slice x0 -> x1, local copies, waits for them, and re-layouts: none -> 3.3 us  [pick(): return lax.dynamic_index_in_dim(groups, group, 1, False)]
    all_gather x1, waiting for transfers between devices: 16.4 us -> 19.6 us  [shards(): lax.all_gather(out_weight, 'pairs', axis=1, tiled=True)]
    and x4, other arithmetic: 3.46 us -> 0.45 us  [shards(): (pair_ids[:, None] == pair_ids[None, :]) & (pair_ids[:, None] < SLOTS)]
    all_to_all x1, waiting for transfers between devices: 23.8 us -> 21.5 us  [shards(): lax.all_to_all(outgoing, 'pairs', split_axis=0, concat_axis=0, tiled=True)]
    unnamed x8 -> x14, local copies, waits for them, and re-layouts: 6.33 us -> 4.35 us
  transfers between devices with their start and end apart: 3 -> 4, of which waited for: 3 -> 4; matrix products, arithmetic and copies ran while one was open for 16% -> 12% of each run, Pallas kernels for 0% -> 0%
where the time goes in v8:
time: 170 us
  waiting for transfers between devices  79.6 us (47%)
  blocking collectives  31.6 us (19%)
  local copies, waits for them, and re-layouts  14.2 us (8%)
  between operations  13.7 us (8%)
  starting transfers between devices  12.3 us (7%)
  matrix products  12 us (7%)
  other arithmetic  6.23 us (4%)
    unnamed x1, blocking collectives  31.6 us
    all_to_all x1, waiting for transfers between devices, shards(): lax.all_to_all(outgoing, 'pairs', split_axis=0, concat_axis=0, tiled=True)  21.5 us
    all_gather x1, waiting for transfers between devices, shards(): lax.all_gather(out_weight, 'pairs', axis=1, tiled=True)  19.6 us
    ppermute x1, waiting for transfers between devices, shards(): lax.ppermute(pair_sums[1], 'tensor', [(0, 3), (3, 0), (1, 2), (2, 1)])  19.4 us
    ppermute x1, waiting for transfers between devices, shards(): came = lax.ppermute(sent, 'tensor', [(0, 1), (1, 0), (2, 3), (3, 2)])  18.4 us
    all_to_all x1, starting transfers between devices, shards(): lax.all_to_all(outgoing, 'pairs', split_axis=0, concat_axis=0, tiled=True)  6.75 us
    dot_general x1, matrix products, shards(): jnp.dot(moved_rows, lax.all_gather(out_weight, 'pairs', axis=1, tiled=Tru...  6.27 us
    unnamed x14, local copies, waits for them, and re-layouts  4.35 us
  transfers between devices with their start and end apart: 4, of which 4 were waited for; matrix products, arithmetic and copies ran while one was open for 12% of the time, Pallas kernels for 0%

profile of v8, /device:TPU:6, one launch (start us, length us, event | category | flops | bytes accessed | tf_op | source)
XLA Modules:
  0.0 169.7 jit_solution(2705152616424425033)
XLA Ops:
  6.5 0.0 all-gather.2.cloned.1.call-start
  6.5 0.7 all-gather.2.cloned.1.call-update
  7.3 1.3 dynamic-slice
  8.6 1.3 convert_reduce_fusion
  9.9 1.4 dynamic-update-slice
  11.3 31.6 %all-reduce = s32[128]{0:T(128)S(1)} all-reduce(s32[128]{0:T(128)S(1)} %dynamic-update-slice), channel_id=1, replica_groups=mesh['pairs'=128,'tensor'=4] {'pairs'}, use_global_device_ids=true, to_apply=%add | all-reduce | flops 128 | bytes 1024
  42.9 0.1 copy.24
  43.0 0.2 reduce-window.9
  43.2 0.1 reduce
  43.3 0.6 and_select_fusion.2
  43.9 0.7 and_select_fusion.1
  44.6 0.1 broadcast_add_fusion
  44.6 0.1 copy.31
  44.8 0.1 add.171
  44.9 0.0 copy-start.3
  44.9 1.3 copy.28
  46.2 0.0 copy-done
  46.2 0.2 copy.29
  46.4 0.0 copy-done.1
  46.4 0.2 copy.30
  46.6 0.0 copy-done.3
  46.6 6.3 %while.11 = (s32[]{:T(128)}, bf16[4,256,4,64]{1,3,2,0:T(8,128)(2,1)S(1)}, bf16[4,256,4,64]{1,3,2,0:T(8,128)(2,1)S(1)}, bf16[4,256,4,64]{1,3,2,0:T(8,128)(2,1)S(1...) while((s32[]{:T(128)}, ...), condition=%wide.region_6.7_spmd.clone, body=%wide.region_3.6_spmd.clone.sunk | while | flops 103221760 | bytes 1134933 | solution.py:44
  46.6 0.1 compare_and_fusion.3
  46.8 0.6 fusion.68
  47.4 0.8 fusion.69
  48.2 0.1 compare_and_fusion.3
  48.3 0.6 fusion.68
  48.9 0.8 fusion.69
  49.8 0.1 compare_and_fusion.3
  49.9 0.6 fusion.68
  50.5 0.8 fusion.69
  51.3 0.1 compare_and_fusion.3
  51.5 0.6 fusion.68
  52.1 0.8 fusion.69
  52.9 0.2 copy.32
  53.1 1.2 gather_fusion
  54.3 0.2 gather.7
  54.5 0.1 compare_and_fusion.1
  54.6 0.1 copy.27
  54.7 1.4 broadcast_select_fusion
  56.2 6.7 %all-to-all-start = ((bf16[128,2,1024]{2,1,0:T(2,128)(2,1)}), bf16[128,2,1024]{2,1,0:T(2,128)(2,1)S(1)}, u32[]{:S(2)}, u32[]{:S(2)}) async-start(bf16[128,2,1024]{2,1,0:T(2,128)(2,1)} %broadcast_select_fusion), calls=%async_computation | async-start | bytes 1048576 | tf_op jit(solution)/shard_map/all_to_all | solution.py:59
  62.9 0.1 copy.26
  63.0 0.1 add.164
  63.2 0.1 copy.25
  63.3 0.2 lt.100
  63.5 21.5 %all-to-all-done = bf16[128,2,1024]{2,1,0:T(2,128)(2,1)S(1)} async-done(((bf16[128,2,1024]{2,1,0:T(2,128)(2,1)}), bf16[128,2,1024]{2,1,0:T(2,128)(2,1)S(1)}, u32[]{:S(2)}, u32[]{:S(2)}) %all-to-all-start) | async-done | bytes 524320 | tf_op jit(solution)/shard_map/all_to_all | solution.py:59
  85.0 0.2 reshape.247
  85.2 1.9 %scatter_custom_fusion = bf16[192,1024]{1,0:T(8,128)(2,1)S(1)} fusion(s32[256]{0:T(256)S(1)} %bitcast.90, bf16[256,1024]{1,0:T(8,128)(2,1)S(1)} %reshape.247, bf16[]{:T(256)} %constant.100.clone.1), kind=kCustom, calls=%fused_computation.41 | custom fusion | bytes 393218 | tf_op jit(solution)/shard_map/scatter | solution.py:66
  87.1 19.6 %all-gather.2.cloned.1.call-done = bf16[1024,4096]{0,1:T(8,128)(2,1)} async-done(((bf16[1024,32]{0,1:T(8,128)(2,1)}), bf16[1024,4096]{0,1:T(8,128)(2,1)}) %all-gather.2.cloned.1.call-update) | async-done | bytes 8388624 | tf_op jit(solution)/shard_map/all_gather | solution.py:71
  106.7 6.3 %convolution_convert_fusion.1 = bf16[192,4096]{1,0:T(8,128)(2,1)S(1)} fusion(bf16[192,1024]{1,0:T(8,128)(2,1)S(1)} %scatter_custom_fusion, bf16[1024,4096]{0,1:T(8,128)(2,1)} %all-gather.2.cloned.1.call-done), kind=kOutput, calls=%fused_computation.28 | convolution fusion | flops 1611399168 | bytes 10354688 | tf_op jit(solution)/shard_map/dot_general | solution.py:69
  113.0 1.2 reshape.234
  114.2 3.3 %constant_dynamic-slice_fusion.3 = (bf16[192,1,1024]{2,1,0:T(2,128)(2,1)S(1)}, bf16[192,1,1024]{2,1,0:T(2,128)(2,1)S(1)}, bf16[192,1,1024]{2,1,0:T(2,128)(2,1)S(1)}, bf16[192,1,1024]{2,1,0:T(2,128)(2,1)S(1)}) fusion(bf16[192,4,1024]{2,1,0:T(4,128)(2,1)S(1)} %reshape.234, s32[]{:T(128)S(6)} %select_n.111, s32[]{:T(128)S(6)} %select_n.114, s32[]{:T(128)S(6)} %select_n.112, ...), kind=kLoop, calls=%fused_computation.64 | loop fusion | bytes 3145744 | tf_op jit(solution)/shard_map/jit(dynamic_index_in_dim)/dynamic_slice | solution.py:80
  117.5 0.3 copy_bitcast_fusion
  117.8 0.1 pad_maximum_fusion
  117.9 2.9 %collective-permute-start = (bf16[2,192,1024]{2,1,0:T(8,128)(2,1)S(1)}, bf16[2,192,1024]{2,1,0:T(8,128)(2,1)S(1)}, u32[]{:S(2)}, u32[]{:S(2)}) collective-permute-start(bf16[2,192,1024]{2,1,0:T(8,128)(2,1)S(1)} %pad_maximum_fusion), channel_id=1, source_target_pairs={{0,1},{1,0},{2,3},{3,2},{4,5},{5,4},{6,7},{7,6},{8,9},{9,8},{10,11... | collective-permute-start | bytes 2359304 | tf_op jit(solution)/shard_map/ppermute | solution.py:83
  120.7 0.3 copy_bitcast_fusion.2
  121.0 18.4 %collective-permute-done = bf16[2,192,1024]{2,1,0:T(8,128)(2,1)S(1)} collective-permute-done((bf16[2,192,1024]{2,1,0:T(8,128)(2,1)S(1)}, bf16[2,192,1024]{2,1,0:T(8,128)(2,1)S(1)}, u32[]{:S(2)}, u32[]{:S(2)}) %collective-permute-start) | collective-permute-done | bytes 786464 | tf_op jit(solution)/shard_map/ppermute | solution.py:83
  139.4 0.3 convert_add_fusion
  139.7 0.0 copy-start.2
  139.7 0.1 slice_bitcast_fusion
  139.8 2.7 %collective-permute-start.1 = (f32[192,1024]{1,0:T(8,128)S(1)}, f32[192,1024]{1,0:T(8,128)S(1)}, u32[]{:S(2)}, u32[]{:S(2)}) collective-permute-start(f32[192,1024]{1,0:T(8,128)S(1)} %slice_bitcast_fusion), channel_id=1, source_target_pairs={{0,3},{3,0},{1,2},{2,1},{4,7},{7,4},{5,6},{6,5},{8,11},{11,8},{9,1... | collective-permute-start | bytes 2359304 | tf_op jit(solution)/shard_map/ppermute | solution.py:86
  142.5 19.4 %collective-permute-done.1 = f32[192,1024]{1,0:T(8,128)S(1)} collective-permute-done((f32[192,1024]{1,0:T(8,128)S(1)}, f32[192,1024]{1,0:T(8,128)S(1)}, u32[]{:S(2)}, u32[]{:S(2)}) %collective-permute-start.1) | collective-permute-done | bytes 786464 | tf_op jit(solution)/shard_map/ppermute | solution.py:86
  161.9 0.0 copy-done.2
  161.9 0.9 add_convert_fusion
  (12 shorter events, 0.1 us)
Async XLA Ops:
  6.5 39.6 %copy-start = (bf16[256,1024]{1,0:T(8,128)(2,1)S(1)}, bf16[256,1024]{1,0:T(8,128)(2,1)}, u32[]{:S(2)}) copy-start(bf16[256,1024]{1,0:T(8,128)(2,1)} %param.8) | copy-start | bytes 1572868
  6.5 39.9 %copy-start.1 = (bf16[256,1024]{1,0:T(8,128)(2,1)S(1)}, bf16[256,1024]{1,0:T(8,128)(2,1)}, u32[]{:S(2)}) copy-start(bf16[256,1024]{1,0:T(8,128)(2,1)} %param.9) | copy-start | bytes 1572868
  6.5 100.2 %all-gather.2.cloned.1.call-start = ((), (), s32[]{:S(2)}) async-start(), calls=%async_computation.1 | async-start | bytes 8454144 | tf_op jit(solution)/shard_map/all_gather | solution.py:71
  44.9 1.7 %copy-start.3 = (s32[256]{0:T(256)S(1)}, s32[256]{0:T(256)}, u32[]{:S(2)}) copy-start(s32[256]{0:T(256)} %param.11) | copy-start | bytes 3076
  56.2 28.8 %all-to-all-start = ((bf16[128,2,1024]{2,1,0:T(2,128)(2,1)}), bf16[128,2,1024]{2,1,0:T(2,128)(2,1)S(1)}, u32[]{:S(2)}, u32[]{:S(2)}) async-start(bf16[128,2,1024]{2,1,0:T(2,128)(2,1)} %broadcast_select_fusion), calls=%async_computation | async-start | bytes 1048576 | tf_op jit(solution)/shard_map/all_to_all | solution.py:59
  117.9 21.6 %collective-permute-start = (bf16[2,192,1024]{2,1,0:T(8,128)(2,1)S(1)}, bf16[2,192,1024]{2,1,0:T(8,128)(2,1)S(1)}, u32[]{:S(2)}, u32[]{:S(2)}) collective-permute-start(bf16[2,192,1024]{2,1,0:T(8,128)(2,1)S(1)} %pad_maximum_fusion), channel_id=1, source_target_pairs={{0,1},{1,0},{2,3},{3,2},{4,5},{5,4},{6,7},{7,6},{8,9},{9,8},{10,11... | collective-permute-start | bytes 2359304 | tf_op jit(solution)/shard_map/ppermute | solution.py:83
  139.7 22.2 %copy-start.2 = (bf16[192,1024]{1,0:T(8,128)(2,1)S(1)}, bf16[192,1024]{1,0:T(8,128)(2,1)}, u32[]{:S(2)}) copy-start(bf16[192,1024]{1,0:T(8,128)(2,1)} %param.13) | copy-start | bytes 1179652
  139.8 22.1 %collective-permute-start.1 = (f32[192,1024]{1,0:T(8,128)S(1)}, f32[192,1024]{1,0:T(8,128)S(1)}, u32[]{:S(2)}, u32[]{:S(2)}) collective-permute-start(f32[192,1024]{1,0:T(8,128)S(1)} %slice_bitcast_fusion), channel_id=1, source_target_pairs={{0,3},{3,0},{1,2},{2,1},{4,7},{7,4},{5,6},{6,5},{8,11},{11,8},{9,1... | collective-permute-start | bytes 2359304 | tf_op jit(solution)/shard_map/ppermute | solution.py:86
Sparse Core Ops, SparseCore 0:
  10.5 96.1 all-gather.1

commit v9 on v4

--- a/solution.py
+++ b/solution.py
@@ -78,7 +78,10 @@
         .transpose(1, 0, 2)
     )
     received = lax.all_to_all(by_group, "tensor", 0, 0, tiled=True)
-    projected = jnp.sum(received.astype(jnp.float32), axis=0).astype(jnp.bfloat16)
+    total = received[0].astype(jnp.float32)
+    for group in range(1, tensor_parts):
+        total = total + received[group].astype(jnp.float32)
+    projected = total.astype(jnp.bfloat16)
     return (residual.astype(jnp.float32) + projected.astype(jnp.float32)).astype(jnp.bfloat16)
 
 

time: 149 us -> 148 us (level)
  no operation moved by 1% of the time
where the time goes in v9:
time: 148 us; the launch traced here: 146 us
  blocking collectives  55.3 us (37%)
  waiting for transfers between devices  41.6 us (28%)
  between operations  13.5 us (9%)
  matrix products  11.9 us (8%)
  local copies, waits for them, and re-layouts  11 us (7%)
  starting transfers between devices  6.79 us (5%)
  other arithmetic  5.91 us (4%)
    unnamed x1, blocking collectives  31.6 us
    all_to_all x1, blocking collectives, shards(): received = lax.all_to_all(by_group, 'tensor', 0, 0, tiled=True)  23.7 us
    all_to_all x1, waiting for transfers between devices, shards(): lax.all_to_all(outgoing, 'pairs', split_axis=0, concat_axis=0, tiled=True)  22.5 us
    all_gather x1, waiting for transfers between devices, shards(): lax.all_gather(out_weight, 'pairs', axis=1, tiled=True)  18.4 us
    all_to_all x1, starting transfers between devices, shards(): lax.all_to_all(outgoing, 'pairs', split_axis=0, concat_axis=0, tiled=True)  6.78 us
    unnamed x10, local copies, waits for them, and re-layouts  6.34 us
    dot_general x1, matrix products, shards(): jnp.dot(moved_rows, lax.all_gather(out_weight, 'pairs', axis=1, tiled=Tru...  6.27 us
    dot_general x4, matrix products, attend_group(): jnp.einsum('hqk,khd->qhd', weights, value_part, preferred_element_type=jn...  3.19 us
  transfers between devices with their start and end apart: 2, of which 2 were waited for; matrix products, arithmetic and copies ran while one was open for 15% of the time, Pallas kernels for 0%

profile of v9, /device:TPU:6, one launch (start us, length us, event | category | flops | bytes accessed | tf_op | source)
XLA Modules:
  0.0 146.1 jit_solution(11814716893781845121)
XLA Ops:
  6.5 0.0 copy-start.1
  6.5 0.0 all-gather.2.cloned.1.call-start
  6.5 0.7 all-gather.2.cloned.1.call-update
  7.3 1.3 dynamic-slice
  8.6 1.3 convert_reduce_fusion
  9.9 1.3 dynamic-update-slice
  11.2 31.6 %all-reduce = s32[128]{0:T(128)S(1)} all-reduce(s32[128]{0:T(128)S(1)} %dynamic-update-slice), channel_id=1, replica_groups=mesh['pairs'=128,'tensor'=4] {'pairs'}, use_global_device_ids=true, to_apply=%add | all-reduce | flops 128 | bytes 1024
  42.8 0.1 copy.22
  42.9 0.2 reduce-window.9
  43.1 0.1 reduce
  43.2 0.6 and_select_fusion.2
  43.8 0.6 and_select_fusion.1
  44.4 0.1 broadcast_add_fusion
  44.4 0.1 copy.29
  44.6 0.1 add.157
  44.7 1.3 copy.26
  45.9 1.2 copy.27
  47.2 1.2 copy.28
  48.4 0.0 copy-done.1
  48.5 6.2 %while.11 = (s32[]{:T(128)}, bf16[4,256,4,64]{1,3,2,0:T(8,128)(2,1)S(1)}, bf16[4,256,4,64]{1,3,2,0:T(8,128)(2,1)S(1)}, bf16[4,256,4,64]{1,3,2,0:T(8,128)(2,1)S(1...) while((s32[]{:T(128)}, ...), condition=%wide.region_6.7_spmd.clone, body=%wide.region_3.6_spmd.clone.sunk | while | flops 103221760 | bytes 1134933 | solution.py:44
  48.5 0.1 compare_and_fusion.3
  48.6 0.6 fusion.68
  49.2 0.8 fusion.69
  50.0 0.1 compare_and_fusion.3
  50.1 0.6 fusion.68
  50.8 0.8 fusion.69
  51.6 0.1 compare_and_fusion.3
  51.7 0.6 fusion.68
  52.3 0.8 fusion.69
  53.1 0.1 compare_and_fusion.3
  53.2 0.6 fusion.68
  53.9 0.8 fusion.69
  54.7 0.2 copy.30
  54.9 1.2 gather_fusion
  56.1 0.2 gather.7
  56.3 0.1 compare_and_fusion.1
  56.4 0.1 copy.25
  56.5 1.4 broadcast_select_fusion
  57.9 6.8 %all-to-all-start = ((bf16[128,2,1024]{2,1,0:T(2,128)(2,1)}), bf16[128,2,1024]{2,1,0:T(2,128)(2,1)S(1)}, u32[]{:S(2)}, u32[]{:S(2)}) async-start(bf16[128,2,1024]{2,1,0:T(2,128)(2,1)} %broadcast_select_fusion), calls=%async_computation | async-start | bytes 1048576 | tf_op jit(solution)/shard_map/all_to_all | solution.py:59
  64.7 0.1 copy.24
  64.8 0.1 add.150
  65.0 0.1 copy.23
  65.1 0.2 lt.81
  65.3 22.5 %all-to-all-done = bf16[128,2,1024]{2,1,0:T(2,128)(2,1)S(1)} async-done(((bf16[128,2,1024]{2,1,0:T(2,128)(2,1)}), bf16[128,2,1024]{2,1,0:T(2,128)(2,1)S(1)}, u32[]{:S(2)}, u32[]{:S(2)}) %all-to-all-start) | async-done | bytes 524320 | tf_op jit(solution)/shard_map/all_to_all | solution.py:59
  87.8 0.2 reshape.252
  88.0 1.8 %scatter_custom_fusion = bf16[192,1024]{1,0:T(8,128)(2,1)S(1)} fusion(s32[256]{0:T(256)S(1)} %bitcast.86, bf16[256,1024]{1,0:T(8,128)(2,1)S(1)} %reshape.252, bf16[]{:T(256)} %constant.74.clone.1), kind=kCustom, calls=%fused_computation.35 | custom fusion | bytes 393218 | tf_op jit(solution)/shard_map/scatter | solution.py:66
  89.7 18.4 %all-gather.2.cloned.1.call-done = bf16[1024,4096]{0,1:T(8,128)(2,1)} async-done(((bf16[1024,32]{0,1:T(8,128)(2,1)}), bf16[1024,4096]{0,1:T(8,128)(2,1)}) %all-gather.2.cloned.1.call-update) | async-done | bytes 8388624 | tf_op jit(solution)/shard_map/all_gather | solution.py:71
  108.1 6.3 %convolution_convert_fusion.1 = bf16[192,4096]{1,0:T(8,128)(2,1)S(1)} fusion(bf16[192,1024]{1,0:T(8,128)(2,1)S(1)} %scatter_custom_fusion, bf16[1024,4096]{0,1:T(8,128)(2,1)} %all-gather.2.cloned.1.call-done), kind=kOutput, calls=%fused_computation.28 | convolution fusion | flops 1611399168 | bytes 10354688 | tf_op jit(solution)/shard_map/dot_general | solution.py:69
  114.4 0.0 copy-start
  114.4 0.1 copy.35
  114.6 23.7 %all_to_all.10 = bf16[4,192,1024]{2,1,0:T(8,128)(2,1)S(1)} all-to-all(bf16[4,192,1024]{2,1,0:T(8,128)(2,1)S(1)} %bitcast.78), channel_id=1, replica_groups=mesh['pairs'=128,'tensor'=4] {'tensor'}, dimensions={0} | all-to-all | bytes 3145728 | tf_op jit(solution)/shard_map/all_to_all | solution.py:80
  138.2 0.0 copy-done
  138.2 1.1 fusion.42
  (10 shorter events, 0.1 us)
Async XLA Ops:
  6.5 41.9 %copy-start.1 = (s32[256]{0:T(256)S(1)}, s32[256]{0:T(256)}, u32[]{:S(2)}) copy-start(s32[256]{0:T(256)} %param.11) | copy-start | bytes 3076
  6.5 101.6 %all-gather.2.cloned.1.call-start = ((), (), s32[]{:S(2)}) async-start(), calls=%async_computation.2 | async-start | bytes 8454144 | tf_op jit(solution)/shard_map/all_gather | solution.py:71
  57.9 29.8 %all-to-all-start = ((bf16[128,2,1024]{2,1,0:T(2,128)(2,1)}), bf16[128,2,1024]{2,1,0:T(2,128)(2,1)S(1)}, u32[]{:S(2)}, u32[]{:S(2)}) async-start(bf16[128,2,1024]{2,1,0:T(2,128)(2,1)} %broadcast_select_fusion), calls=%async_computation | async-start | bytes 1048576 | tf_op jit(solution)/shard_map/all_to_all | solution.py:59
  114.4 23.8 %copy-start = (bf16[192,1024]{1,0:T(8,128)(2,1)S(1)}, bf16[192,1024]{1,0:T(8,128)(2,1)}, u32[]{:S(2)}) copy-start(bf16[192,1024]{1,0:T(8,128)(2,1)} %param.13) | copy-start | bytes 1179652
Sparse Core Ops, SparseCore 0:
  10.5 97.5 all-gather.1

commit v10 on v4

--- a/solution.py
+++ b/solution.py
@@ -66,17 +66,14 @@
     moved_rows = landed.at[incoming_slots.reshape(-1)].set(
         incoming.reshape(-1, local_width), mode="drop"
     )
-    partial_value = jnp.dot(
+    tensor_parts = lax.axis_size("tensor")
+    group_weight = lax.all_gather(out_weight, "pairs", axis=1, tiled=True)
+    by_group = jnp.einsum(
+        "rk,kgn->grn",
         moved_rows,
-        lax.all_gather(out_weight, "pairs", axis=1, tiled=True),
+        group_weight.reshape(local_width, tensor_parts, local_width),
         preferred_element_type=jnp.float32,
-    )
-    tensor_parts = lax.axis_size("tensor")
-    by_group = (
-        partial_value.astype(jnp.bfloat16)
-        .reshape(balanced_rows, tensor_parts, local_width)
-        .transpose(1, 0, 2)
-    )
+    ).astype(jnp.bfloat16)
     received = lax.all_to_all(by_group, "tensor", 0, 0, tiled=True)
     projected = jnp.sum(received.astype(jnp.float32), axis=0).astype(jnp.bfloat16)
     return (residual.astype(jnp.float32) + projected.astype(jnp.float32)).astype(jnp.bfloat16)

time: 149 us -> 151 us (1.013)
  other arithmetic: 6.04 us -> 9.05 us
    and x4, other arithmetic: 0.44 us -> 3.46 us  [shards(): (pair_ids[:, None] == pair_ids[None, :]) & (pair_ids[:, None] < SLOTS)]
    all_gather x1, waiting for transfers between devices: 18.4 us -> 16.4 us  [shards(): group_weight = lax.all_gather(out_weight, 'pairs', axis=1, tiled=True)]
    unnamed x10 -> x8, local copies, waits for them, and re-layouts: 6.34 us -> 6.33 us
  transfers between devices with their start and end apart: 2 -> 2, of which waited for: 2 -> 2; matrix products, arithmetic and copies ran while one was open for 15% -> 16% of each run, Pallas kernels for 0% -> 0%
where the time goes in v10:
time: 151 us; the launch traced here: 149 us
  blocking collectives  55.3 us (37%)
  waiting for transfers between devices  41 us (27%)
  between operations  13.5 us (9%)
  matrix products  11.9 us (8%)
  local copies, waits for them, and re-layouts  10.9 us (7%)
  other arithmetic  9.05 us (6%)
  starting transfers between devices  6.79 us (4%)
    unnamed x1, blocking collectives  31.6 us
    all_to_all x1, waiting for transfers between devices, shards(): lax.all_to_all(outgoing, 'pairs', split_axis=0, concat_axis=0, tiled=True)  23.9 us
    all_to_all x1, blocking collectives, shards(): received = lax.all_to_all(by_group, 'tensor', 0, 0, tiled=True)  23.7 us
    all_gather x1, waiting for transfers between devices, shards(): group_weight = lax.all_gather(out_weight, 'pairs', axis=1, tiled=True)  16.4 us
    all_to_all x1, starting transfers between devices, shards(): lax.all_to_all(outgoing, 'pairs', split_axis=0, concat_axis=0, tiled=True)  6.79 us
    unnamed x8, local copies, waits for them, and re-layouts  6.33 us
    dot_general x1, matrix products, shards(): jnp.einsum('rk,kgn->grn', moved_rows, group_weight.reshape(local_width, t...  6.28 us
    and x4, other arithmetic, shards(): (pair_ids[:, None] == pair_ids[None, :]) & (pair_ids[:, None] < SLOTS)  3.46 us
  transfers between devices with their start and end apart: 2, of which 2 were waited for; matrix products, arithmetic and copies ran while one was open for 16% of the time, Pallas kernels for 0%

profile of v10, /device:TPU:6, one launch (start us, length us, event | category | flops | bytes accessed | tf_op | source)
XLA Modules:
  0.0 148.6 jit_solution(18279819164599025737)
XLA Ops:
  6.5 0.0 all-gather.2.cloned.1.call-start
  6.5 0.7 all-gather.2.cloned.1.call-update
  7.3 1.3 dynamic-slice
  8.6 1.3 convert_reduce_fusion
  9.9 1.3 dynamic-update-slice
  11.2 31.6 %all-reduce = s32[128]{0:T(128)S(1)} all-reduce(s32[128]{0:T(128)S(1)} %dynamic-update-slice), channel_id=1, replica_groups=mesh['pairs'=128,'tensor'=4] {'pairs'}, use_global_device_ids=true, to_apply=%add | all-reduce | flops 128 | bytes 1024
  42.8 0.1 copy.21
  42.9 0.2 reduce-window.9
  43.1 0.1 reduce.1
  43.2 0.6 and_select_fusion.2
  43.8 0.6 and_select_fusion.1
  44.4 0.1 broadcast_add_fusion
  44.4 0.1 copy.28
  44.6 0.1 add.143
  44.7 1.3 copy.25
  45.9 1.2 copy.26
  47.2 1.2 copy.27
  48.4 9.2 %while.11 = (s32[]{:T(128)}, bf16[4,256,4,64]{1,3,2,0:T(8,128)(2,1)S(1)}, bf16[4,256,4,64]{1,3,2,0:T(8,128)(2,1)S(1)}, bf16[4,256,4,64]{1,3,2,0:T(8,128)(2,1)S(1...) while((s32[]{:T(128)}, ...), condition=%wide.region_6.7_spmd.clone, body=%wide.region_3.6_spmd.clone.sunk | while | flops 103221760 | bytes 1134933 | solution.py:44
  48.5 0.9 compare_and_fusion.3
  49.3 0.6 fusion.67
  50.0 0.8 fusion.68
  50.8 0.9 compare_and_fusion.3
  51.6 0.6 fusion.67
  52.3 0.8 fusion.68
  53.1 0.9 compare_and_fusion.3
  53.9 0.6 fusion.67
  54.6 0.8 fusion.68
  55.4 0.9 compare_and_fusion.3
  56.3 0.6 fusion.67
  56.9 0.8 fusion.68
  57.7 0.2 copy.29
  57.9 1.2 gather_fusion
  59.1 0.2 gather.7
  59.3 0.1 compare_and_fusion.1
  59.4 0.1 copy.24
  59.5 1.4 broadcast_select_fusion
  60.9 6.8 %all-to-all-start = ((bf16[128,2,1024]{2,1,0:T(2,128)(2,1)}), bf16[128,2,1024]{2,1,0:T(2,128)(2,1)S(1)}, u32[]{:S(2)}, u32[]{:S(2)}) async-start(bf16[128,2,1024]{2,1,0:T(2,128)(2,1)} %broadcast_select_fusion), calls=%async_computation | async-start | bytes 1048576 | tf_op jit(solution)/shard_map/all_to_all | solution.py:59
  67.7 0.1 copy.23
  67.9 0.1 add.136
  68.0 0.1 copy.22
  68.1 0.2 lt.81
  68.3 0.0 copy-start
  68.3 23.9 %all-to-all-done = bf16[128,2,1024]{2,1,0:T(2,128)(2,1)S(1)} async-done(((bf16[128,2,1024]{2,1,0:T(2,128)(2,1)}), bf16[128,2,1024]{2,1,0:T(2,128)(2,1)S(1)}, u32[]{:S(2)}, u32[]{:S(2)}) %all-to-all-start) | async-done | bytes 524320 | tf_op jit(solution)/shard_map/all_to_all | solution.py:59
  92.2 0.2 reshape.243
  92.4 1.8 %scatter_custom_fusion = bf16[192,1024]{1,0:T(8,128)(2,1)S(1)} fusion(s32[256]{0:T(256)S(1)} %bitcast.77, bf16[256,1024]{1,0:T(8,128)(2,1)S(1)} %reshape.243, bf16[]{:T(256)} %constant.76.clone.1), kind=kCustom, calls=%fused_computation.33 | custom fusion | bytes 393218 | tf_op jit(solution)/shard_map/scatter | solution.py:66
  94.1 16.4 %all-gather.2.cloned.1.call-done = bf16[1024,4096]{0,1:T(8,128)(2,1)} async-done(((bf16[1024,32]{0,1:T(8,128)(2,1)}), bf16[1024,4096]{0,1:T(8,128)(2,1)}) %all-gather.2.cloned.1.call-update) | async-done | bytes 8388624 | tf_op jit(solution)/shard_map/all_gather | solution.py:70
  110.6 6.3 %fusion.42 = bf16[4,192,1024]{2,1,0:T(8,128)(2,1)S(1)} fusion(bf16[1024,4,1024]{0,2,1:T(8,128)(2,1)} %bitcast.78, bf16[192,1024]{1,0:T(8,128)(2,1)S(1)} %scatter_custom_fusion), kind=kOutput, calls=%fused_computation.29 | convolution fusion | flops 1611399168 | bytes 10354688 | tf_op jit(solution)/shard_map/rk,kgn->grn/dot_general | solution.py:71
  116.9 23.7 %all_to_all.10 = bf16[4,192,1024]{2,1,0:T(8,128)(2,1)S(1)} all-to-all(bf16[4,192,1024]{2,1,0:T(8,128)(2,1)S(1)} %fusion.42), channel_id=1, replica_groups=mesh['pairs'=128,'tensor'=4] {'tensor'}, dimensions={0} | all-to-all | bytes 3145728 | tf_op jit(solution)/shard_map/all_to_all | solution.py:77
  140.5 0.3 reduce_sum.41
  140.8 0.0 copy-done
  140.8 0.9 add_convert_fusion
  (10 shorter events, 0.1 us)
Async XLA Ops:
  6.5 104.0 %all-gather.2.cloned.1.call-start = ((), (), s32[]{:S(2)}) async-start(), calls=%async_computation.2 | async-start | bytes 8454144 | tf_op jit(solution)/shard_map/all_gather | solution.py:70
  60.9 31.2 %all-to-all-start = ((bf16[128,2,1024]{2,1,0:T(2,128)(2,1)}), bf16[128,2,1024]{2,1,0:T(2,128)(2,1)S(1)}, u32[]{:S(2)}, u32[]{:S(2)}) async-start(bf16[128,2,1024]{2,1,0:T(2,128)(2,1)} %broadcast_select_fusion), calls=%async_computation | async-start | bytes 1048576 | tf_op jit(solution)/shard_map/all_to_all | solution.py:59
  68.3 72.5 %copy-start = (bf16[192,1024]{1,0:T(8,128)(2,1)S(1)}, bf16[192,1024]{1,0:T(8,128)(2,1)}, u32[]{:S(2)}) copy-start(bf16[192,1024]{1,0:T(8,128)(2,1)} %param.13) | copy-start | bytes 1179652
Sparse Core Ops, SparseCore 0:
  10.5 100.0 all-gather.1
